TPU v7x, 512 devices: a whole 4x8x8 slice. The times are simulated.
512 devices in a mesh: dp: 8 (over y), seq: 64 (over z, x, core).
Axes of the slice: x: 4, y: 8, z: 8, core: 2. Of those that a mesh axis runs over, the one named last changes fastest.
Arguments:
- queries: bfloat16 [8, 8192, 2048], P('dp', 'seq'), may hold values from -6 to 6
- keys: bfloat16 [8, 8192, 2048], P('dp', 'seq'), may hold values from -6 to 6
- values: bfloat16 [8, 8192, 2048], P('dp', 'seq'), may hold values from -6 to 6
- lengths: int32 [8], P('dp'), may hold values from 2048 to 8192, as said below
- norm_gain: float32 [2048], replicated, may hold values from 0.1 to 1.9
- out_weight: bfloat16 [2048, 2048], P('seq', 'dp'), may hold values from -0.125 to 0.125
Outputs:
- projected: bfloat16 [8, 8192, 2048], P('dp', 'seq')
Inputs may be any that keep to these rules, and one draw needn't show every extreme that they name: `lengths`: each length is a multiple of 128; in every draw some document has the full 8192 tokens.
All inputs are finite; a program needn't handle non-finite values.
Results may differ from a plain program's by a relative error of at most 0.005.
Values may be sent and summed in bfloat16 or wider, within the bound.
No kernel may reach another device: no remote copies, remote signals or barrier semaphores. Data moves between devices by JAX's collectives and lax.ppermute only.
A program may use at most 192 MiB of HBM per device.

v0:
```python
import jax
import jax.numpy as jnp
from jax import lax
from jax.sharding import PartitionSpec as P

HEADS = 16
HEAD = 128
BLOCK = 128


def entering(x, axis, combine, identity):
    length, index = (lax.axis_size(axis), lax.axis_index(axis))
    everything = lax.all_gather(x, axis)
    start = jnp.broadcast_to(jnp.asarray(identity, x.dtype), x.shape)

    def lap(k, before):
        reached = k < index
        new = combine(before, everything[k])
        return jnp.where(reached, new, before)

    return lax.fori_loop(0, length, lap, start)


def combine_states(earlier, later):
    return earlier + later


def body(queries, keys, values, lengths, norm_gain, out_weight):
    query_doc = queries[0]
    tok = query_doc.shape[0]
    nblk = tok // BLOCK
    shape = (nblk, BLOCK, HEADS, HEAD)
    query_blocks = query_doc.reshape(shape)
    key_blocks = keys[0].reshape(shape)
    value_blocks = values[0].reshape(shape)
    high = lax.Precision.HIGHEST
    block_state = jnp.einsum(
        "nshd,nshe->nhde", key_blocks, value_blocks, preferred_element_type=jnp.float32
    )
    own_state = jnp.sum(block_state, axis=0)
    zero_state = jnp.zeros((HEADS, HEAD, HEAD), jnp.float32)
    prefix = entering(own_state, "seq", combine_states, zero_state)
    running = jnp.cumsum(block_state, axis=0)
    earlier = jnp.concatenate(
        [jnp.zeros((1, HEADS, HEAD, HEAD), jnp.float32), running[:-1]], axis=0
    )
    prior_state = prefix[None] + earlier
    causal = jnp.arange(BLOCK)[:, None] >= jnp.arange(BLOCK)[None, :]
    scores = jnp.einsum(
        "nthd,nshd->nhts", query_blocks, key_blocks, preferred_element_type=jnp.float32
    )
    scores = jnp.where(causal[None, None], scores, 0.0).astype(jnp.bfloat16)
    local = jnp.einsum("nhts,nshd->nthd", scores, value_blocks, preferred_element_type=jnp.float32)
    cross = jnp.einsum(
        "nthd,nhde->nthe", query_blocks.astype(jnp.float32), prior_state, precision=high
    )
    mixed = (local + cross).reshape(tok, HEADS, HEAD)
    meansq = jnp.mean(mixed * mixed, axis=-1, keepdims=True)
    normed = mixed * lax.rsqrt(meansq + 1e-06) * norm_gain.reshape(HEADS, HEAD)
    position = lax.axis_index("seq") * tok + jnp.arange(tok)
    valid = position < lengths[0]
    normed = jnp.where(valid[:, None, None], normed, 0.0).astype(jnp.bfloat16)
    normed = normed.reshape(tok, HEADS * HEAD)
    wide_rows = lax.all_gather(out_weight, "dp", axis=1, tiled=True)
    full_weight = lax.all_gather(wide_rows, "seq", axis=0, tiled=True)
    result = jnp.dot(normed, full_weight, preferred_element_type=jnp.float32)
    return result.astype(jnp.bfloat16)[None]


def solution(mesh):
    in_specs = (
        P("dp", "seq", None),
        P("dp", "seq", None),
        P("dp", "seq", None),
        P("dp"),
        P(),
        P("seq", "dp"),
    )
    out_specs = P("dp", "seq", None)
    return jax.shard_map(body, mesh=mesh, in_specs=in_specs, out_specs=out_specs, check_vma=False)
```

profile of v0, /device:TPU:1, one launch (start us, length us, event | category | flops | bytes accessed | tf_op | source)
XLA Modules:
  0.0 376.5 jit_solution(2291145478598790153)
XLA Ops:
  10.4 22.8 %all_gather.11 = bf16[32,2048]{1,0:T(8,128)(2,1)} all-gather(bf16[32,256]{1,0:T(8,128)(2,1)} %param.13), channel_id=1, replica_groups=mesh['dp'=8,'seq'=64] {'dp'}, dimensions={1}, use_global_device_ids=true | all-gather | bytes 147456 | tf_op jit(solution)/shard_map/all_gather | solution.py:64
  35.2 1.6 convolution_bitcast_fusion
  36.8 222.1 %all-gather.6.cloned.1.call-done = f32[1024,128,128]{2,1,0:T(8,128)} async-done(((f32[16,128,128]{2,1,0:T(8,128)}), f32[1024,128,128]{2,1,0:T(8,128)}) %all-gather.6.cloned.1.call-update) | async-done | bytes 67108880 | tf_op jit(solution)/shard_map/all_gather | solution.py:13
  258.9 103.9 %while.14 = (s32[]{:T(128)}, f32[16,128,128]{2,1,0:T(8,128)S(1)}, s32[]{:T(128)}, f32[64,16,128,128]{3,2,1,0:T(8,128)}, s32[]{:T(128)}, /*index=5*/s32[]{:T(128)}) while((s32[]{:T(128)}, f32[16,128,128]{2,1,0:T(8,128)S(1)}, s32[]{:T(128)}, f32[64,16,128,128]{3,2,1,0:T(8,128)}, s32[]{:T(128)}, /*index=5*/s32[]{:T(128)}) %tuple.33), condition=%wide.region_1.2_spmd.clone, body=%wide.region_0.0_spmd.clone.sunk | while | flops 786436 | bytes 3145821 | solution.py:21
  258.9 1.6 add_select_fusion.2
  260.5 1.6 add_select_fusion.2
  262.1 1.6 add_select_fusion.2
  265.4 1.6 add_select_fusion.2
  268.6 1.6 add_select_fusion.2
  271.8 1.6 add_select_fusion.2
  273.4 1.6 add_select_fusion.2
  276.7 1.6 add_select_fusion.2
  279.9 1.6 add_select_fusion.2
  283.1 1.6 add_select_fusion.2
  284.8 1.6 add_select_fusion.2
  286.4 1.6 add_select_fusion.2
  288.0 1.6 add_select_fusion.2
  291.2 1.6 add_select_fusion.2
  292.8 1.6 add_select_fusion.2
  294.4 1.6 add_select_fusion.2
  296.1 1.6 add_select_fusion.2
  297.7 1.6 add_select_fusion.2
  299.3 1.6 add_select_fusion.2
  300.9 1.6 add_select_fusion.2
  304.1 1.6 add_select_fusion.2
  307.4 1.6 add_select_fusion.2
  310.6 1.6 add_select_fusion.2
  313.8 1.6 add_select_fusion.2
  317.0 1.6 add_select_fusion.2
  318.7 1.7 add_select_fusion.2
  320.4 1.6 add_select_fusion.2
  322.0 1.6 add_select_fusion.2
  323.6 1.6 add_select_fusion.2
  325.2 1.6 add_select_fusion.2
  326.9 1.6 add_select_fusion.2
  328.5 1.8 add_select_fusion.2
  330.3 1.6 add_select_fusion.2
  331.9 1.6 add_select_fusion.2
  333.6 1.6 add_select_fusion.2
  335.2 1.6 add_select_fusion.2
  336.8 1.6 add_select_fusion.2
  338.5 1.6 add_select_fusion.2
  340.1 1.6 add_select_fusion.2
  341.8 1.6 add_select_fusion.2
  343.4 1.6 add_select_fusion.2
  345.0 1.6 add_select_fusion.2
  346.7 1.6 add_select_fusion.2
  364.2 5.5 %fusion = bf16[1,128,2048]{2,1,0:T(8,128)(2,1)} fusion(bf16[128,2048]{0,1:T(8,128)(2,1)S(1)} %fusion.4, bf16[2048,2048]{1,0:T(8,128)(2,1)} %all-gather.4.cloned.1.call-done), kind=kOutput, calls=%fused_computation.2 | convolution fusion | flops 1074003968 | bytes 9437184 | tf_op jit(solution)/shard_map/dot_general | solution.py:66
  (40 shorter events, 39.9 us)
Async XLA Ops:
  6.5 252.4 %all-gather.6.cloned.1.call-start = ((), (), s32[]{:S(2)}) async-start(), calls=%async_computation.1 | async-start | bytes 68157440 | tf_op jit(solution)/shard_map/all_gather | solution.py:13
  10.4 353.9 %all-gather.4.cloned.1.call-start = ((), (), s32[]{:S(2)}) async-start(), calls=%async_computation | async-start | bytes 8519680 | tf_op jit(solution)/shard_map/all_gather | solution.py:65
  36.8 326.0 %copy-start = (f32[16,128,128]{2,1,0:T(8,128)S(1)}, f32[16,128,128]{2,1,0:T(8,128)}, u32[]{:S(2)}) copy-start(f32[16,128,128]{2,1,0:T(8,128)} %convolution_bitcast_fusion) | copy-start | bytes 3145732
  258.9 105.0 %copy-start.1 = (f32[2048]{0:T(1024)S(1)}, f32[2048]{0:T(1024)}, u32[]{:S(2)}) copy-start(f32[2048]{0:T(1024)} %param.12) | copy-start | bytes 24580
Sparse Core Ops, SparseCore 0:
  10.7 248.1 all-gather.5
  262.2 85.6 all-gather.3
where the time goes:
time: 379 us; the launch traced here: 377 us
  waiting for transfers between devices  222 us (59%)
  other arithmetic  103 us (27%)
  blocking collectives  22.8 us (6%)
  between operations  14.2 us (4%)
  matrix products  9.43 us (2%)
    all_gather x1, waiting for transfers between devices, entering(): everything = lax.all_gather(x, axis)  222 us
    select_n x64, other arithmetic, lap(): return jnp.where(reached, new, before)  102 us
    all_gather x1, blocking collectives, body(): wide_rows = lax.all_gather(out_weight, 'dp', axis=1, tiled=True)  22.8 us
  transfers between devices with their start and end apart: 2, of which 1 were waited for; matrix products, arithmetic and copies ran while one was open for 28% of the time, Pallas kernels for 0%

commit v1 on v0

v1 whole, which is shorter than its diff:
```python
import jax
import jax.numpy as jnp
import numpy as np
from jax import lax
from jax.sharding import Mesh
from jax.sharding import PartitionSpec as P

HEADS = 16
HEAD = 128
BLOCK = 128

SEQ_AXES = ("z", "x", "c")


def exclusive_sum(stack, index):
    mask = jnp.arange(stack.shape[0]) < index
    mask = mask.reshape((-1,) + (1,) * (stack.ndim - 1))
    return jnp.sum(jnp.where(mask, stack, 0.0), axis=0)


def prefix_of(own):
    zi, xi, ci = (lax.axis_index(a) for a in SEQ_AXES)
    nx, nc = lax.axis_size("x"), lax.axis_size("c")
    on_chip = lax.all_gather(own, "c")
    chip_total = jnp.sum(on_chip, axis=0)
    within_chip = exclusive_sum(on_chip, ci)
    half = HEADS // nc
    mine = lax.dynamic_slice_in_dim(chip_total, ci * half, half, 0)
    row = lax.all_gather(mine, "x")
    before_in_row = exclusive_sum(row, xi)
    row_total = jnp.sum(row, axis=0)
    quarter = half // nx
    piece = lax.dynamic_slice_in_dim(row_total, xi * quarter, quarter, 0)
    rows = lax.all_gather(piece, "z")
    before_rows = exclusive_sum(rows, zi)
    before_rows = lax.all_gather(before_rows, "x", axis=0, tiled=True)
    chip_prefix = lax.all_gather(before_rows + before_in_row, "c", axis=0, tiled=True)
    return chip_prefix + within_chip


def body(queries, keys, values, lengths, norm_gain, out_weight):
    nz, nx, nc = (lax.axis_size(a) for a in SEQ_AXES)
    query_doc = queries[0]
    tok = query_doc.shape[0]
    nblk = tok // BLOCK
    shape = (nblk, BLOCK, HEADS, HEAD)
    query_blocks = query_doc.reshape(shape)
    key_blocks = keys[0].reshape(shape)
    value_blocks = values[0].reshape(shape)
    high = lax.Precision.HIGHEST
    block_state = jnp.einsum(
        "nshd,nshe->nhde", key_blocks, value_blocks, preferred_element_type=jnp.float32
    )
    own_state = jnp.sum(block_state, axis=0)
    prefix = prefix_of(own_state)
    running = jnp.cumsum(block_state, axis=0)
    earlier = jnp.concatenate(
        [jnp.zeros((1, HEADS, HEAD, HEAD), jnp.float32), running[:-1]], axis=0
    )
    prior_state = prefix[None] + earlier
    causal = jnp.arange(BLOCK)[:, None] >= jnp.arange(BLOCK)[None, :]
    scores = jnp.einsum(
        "nthd,nshd->nhts", query_blocks, key_blocks, preferred_element_type=jnp.float32
    )
    scores = jnp.where(causal[None, None], scores, 0.0).astype(jnp.bfloat16)
    local = jnp.einsum("nhts,nshd->nthd", scores, value_blocks, preferred_element_type=jnp.float32)
    cross = jnp.einsum(
        "nthd,nhde->nthe", query_blocks.astype(jnp.float32), prior_state, precision=high
    )
    mixed = (local + cross).reshape(tok, HEADS, HEAD)
    meansq = jnp.mean(mixed * mixed, axis=-1, keepdims=True)
    normed = mixed * lax.rsqrt(meansq + 1e-06) * norm_gain.reshape(HEADS, HEAD)
    seq_index = lax.axis_index(SEQ_AXES)
    position = seq_index * tok + jnp.arange(tok)
    valid = position < lengths[0]
    normed = jnp.where(valid[:, None, None], normed, 0.0).astype(jnp.bfloat16)
    rows_per, cols_per = out_weight.shape
    ndp = lax.axis_size("dp")
    gathered = lax.all_gather(out_weight, ("dp", "z", "x"), axis=0)
    gathered = gathered.reshape(ndp, nz, nx, rows_per, cols_per)
    weight = lax.all_gather(gathered, "c", axis=0)
    normed = normed.reshape(tok, nz, nx, nc, rows_per)
    result = jnp.einsum(
        "tzxcr,cdzxrk->tdk", normed, weight, preferred_element_type=jnp.float32
    )
    return result.astype(jnp.bfloat16).reshape(tok, ndp * cols_per)[None]


def solution(mesh, nx=4, ncore=2):
    ndp, nseq = mesh.devices.shape
    devices = np.asarray(mesh.devices).reshape(ndp, nseq // (nx * ncore), nx, ncore)
    fine = Mesh(devices, ("dp",) + SEQ_AXES)
    rows = P("dp", SEQ_AXES, None)
    in_specs = (rows, rows, rows, P("dp"), P(), P(SEQ_AXES, "dp"))
    return jax.shard_map(body, mesh=fine, in_specs=in_specs, out_specs=rows, check_vma=False)
```

time: 379 us -> 311 us (0.82)
  other arithmetic: 103 us -> 6.6 us
  waiting for transfers between devices: 222 us -> 263 us
  blocking collectives: 22.8 us -> 10.2 us
    select_n x64 -> x0, other arithmetic: 102 us -> none  [lap(): return jnp.where(reached, new, before)]
    all_gather x2 -> x6, waiting for transfers between devices: 222 us -> 262 us  [the longest x1 118 us: body(): gathered = lax.all_gather(out_weight, ('dp', 'z', 'x'), axis=0)]
    all_gather x1, blocking collectives: 22.8 us -> 10.2 us  [prefix_of(): before_rows = lax.all_gather(before_rows, 'x', axis=0, tiled=True)]
    reduce_sum x0 -> x3, other arithmetic: none -> 5.68 us  [exclusive_sum(): return jnp.sum(jnp.where(mask, stack, 0.0), axis=0)]
  transfers between devices with their start and end apart: 2 -> 6, of which waited for: 1 -> 6; matrix products, arithmetic and copies ran while one was open for 28% -> 2% of each run, Pallas kernels for 0% -> 0%
where the time goes in v1:
time: 311 us
  waiting for transfers between devices  263 us (85%)
  between operations  14.3 us (5%)
  matrix products  10.2 us (3%)
  blocking collectives  10.2 us (3%)
  other arithmetic  6.6 us (2%)
  local copies, waits for them, and re-layouts  6.49 us (2%)
    all_gather x1, waiting for transfers between devices, body(): gathered = lax.all_gather(out_weight, ('dp', 'z', 'x'), axis=0)  118 us
    all_gather x1, waiting for transfers between devices, prefix_of(): rows = lax.all_gather(piece, 'z')  37 us
    all_gather x1, waiting for transfers between devices, prefix_of(): row = lax.all_gather(mine, 'x')  35.9 us
    all_gather x1, waiting for transfers between devices, body(): weight = lax.all_gather(gathered, 'c', axis=0)  28.7 us
    all_gather x1, waiting for transfers between devices, prefix_of(): on_chip = lax.all_gather(own, 'c')  25.7 us
    all_gather x1, waiting for transfers between devices, prefix_of(): lax.all_gather(before_rows + before_in_row, 'c', axis=0, tiled=True)  16.7 us
    all_gather x1, blocking collectives, prefix_of(): before_rows = lax.all_gather(before_rows, 'x', axis=0, tiled=True)  10.2 us
  transfers between devices with their start and end apart: 6, of which 6 were waited for; matrix products, arithmetic and copies ran while one was open for 2% of the time, Pallas kernels for 0%

profile of v1, /device:TPU:1, one launch (start us, length us, event | category | flops | bytes accessed | tf_op | source)
XLA Modules:
  0.0 310.6 jit_solution(10044616053347332183)
XLA Ops:
  6.5 0.0 all-gather.15.cloned.1.call-start
  6.5 1.3 copy.51
  7.9 1.1 copy.53
  9.0 1.3 fusion.23
  10.3 0.0 all-gather.15.cloned.1.call-update
  10.3 0.0 all-gather.17.cloned.1.call-start
  10.4 25.7 %all-gather.15.cloned.1.call-done = f32[32,128,128]{2,1,0:T(8,128)} async-done(((f32[16,128,128]{2,1,0:T(8,128)}), f32[32,128,128]{2,1,0:T(8,128)}) %all-gather.15.cloned.1.call-update) | async-done | bytes 2097168 | tf_op jit(solution)/shard_map/all_gather | solution.py:24
  36.1 2.3 select_reduce_fusion
  38.4 0.8 constant_dynamic-slice_fusion.1
  39.2 0.0 all-gather.17.cloned.1.call-update
  39.3 0.0 all-gather.19.cloned.1.call-start
  39.3 35.9 %all-gather.17.cloned.1.call-done = f32[32,128,128]{2,1,0:T(8,128)} async-done(((f32[8,128,128]{2,1,0:T(8,128)}), f32[32,128,128]{2,1,0:T(8,128)}) %all-gather.17.cloned.1.call-update) | async-done | bytes 2097168 | tf_op jit(solution)/shard_map/all_gather | solution.py:29
  75.2 2.0 select_reduce_fusion.1
  77.2 0.7 constant_dynamic-slice_fusion
  77.9 0.0 all-gather.19.cloned.1.call-update
  77.9 0.0 all-gather.21.cloned.1.call-start
  78.0 0.5 all-gather.21.cloned.1.call-update
  78.5 0.0 all-gather.11.cloned.1.call-start
  78.6 37.0 %all-gather.19.cloned.1.call-done = f32[16,128,128]{2,1,0:T(8,128)} async-done(((f32[2,128,128]{2,1,0:T(8,128)}), f32[16,128,128]{2,1,0:T(8,128)}) %all-gather.19.cloned.1.call-update) | async-done | bytes 1048592 | tf_op jit(solution)/shard_map/all_gather | solution.py:34
  115.6 1.4 select_reduce_fusion.2
  117.0 10.2 %all_gather.36 = f32[8,128,128]{2,1,0:T(8,128)S(1)} all-gather(f32[2,128,128]{2,1,0:T(8,128)S(1)} %select_reduce_fusion.2), channel_id=1, replica_groups=mesh['dp'=8,'z'=8,'x'=4,'c'=2] {'x'}, dimensions={0}, use_global_device_ids=true | all-gather | bytes 655360 | tf_op jit(solution)/shard_map/all_gather | solution.py:36
  127.2 0.9 add.54
  128.0 0.0 all-gather.11.cloned.1.call-update
  128.1 0.0 all-gather.13.cloned.1.call-start
  128.1 118.0 %all-gather.21.cloned.1.call-done = bf16[8192,256]{1,0:T(8,128)(2,1)} async-done(((bf16[32,256]{1,0:T(8,128)(2,1)}), bf16[8192,256]{1,0:T(8,128)(2,1)}) %all-gather.21.cloned.1.call-update) | async-done | bytes 4194320 | tf_op jit(solution)/shard_map/all_gather | solution.py:79
  246.1 0.0 copy-start
  246.1 0.0 copy-start.1
  246.1 0.0 all-gather.13.cloned.1.call-update
  246.2 1.0 copy-done
  247.2 0.1 copy.52
  248.0 0.0 copy-done.1
  248.0 0.1 mul.50
  248.1 1.6 convolution_bitcast_fusion
  249.7 16.7 %all-gather.11.cloned.1.call-done = f32[16,128,128]{2,1,0:T(8,128)} async-done(((f32[8,128,128]{2,1,0:T(8,128)}), f32[16,128,128]{2,1,0:T(8,128)}) %all-gather.11.cloned.1.call-update) | async-done | bytes 1048592 | tf_op jit(solution)/shard_map/all_gather | solution.py:37
  266.4 2.6 fusion.9
  269.1 28.7 %all-gather.13.cloned.1.call-done = bf16[2,8,8,4,32,256]{5,4,3,2,1,0:T(8,128)(2,1)} async-done(((bf16[1,8,8,4,32,256]{5,4,3,2,1,0:T(8,128)(2,1)}), bf16[2,8,8,4,32,256]{5,4,3,2,1,0:T(8,128)(2,1)}) %all-gather.13.cloned.1.call-update) | async-done | bytes 8388624 | tf_op jit(solution)/shard_map/all_gather | solution.py:81
  297.7 4.7 %fusion.6 = bf16[128,8,256]{2,0,1:T(8,128)(2,1)S(1)} fusion(bf16[2,8,8,4,32,256]{5,4,3,2,1,0:T(8,128)(2,1)} %all-gather.13.cloned.1.call-done, f32[128,8,4,2,32]{0,4,3,2,1:T(8,128)S(1)} %bitcast.49, f32[8,4,2,32]{3,0,1,2:T(8,128)S(1)} %copy.44, f32[128,8,4]{0,1,2:T(8,128)S(1)} %copy.42, pred[128]{0:T(512)(128)(4,1)S(1)} %add_compare_fusion), kind=kOutput, calls=%fused_computation.9 | convolution fusion | flops 1075052544 | bytes 9986176 | tf_op jit(solution)/shard_map/tzxcr,cdzxrk->tdk/dot_general | solution.py:83
  302.5 0.3 copy.46
  302.7 1.0 copy.47
  (9 shorter events, 0.1 us)
Async XLA Ops:
  6.5 29.6 %all-gather.15.cloned.1.call-start = ((), (), s32[]{:S(2)}) async-start(), calls=%async_computation.2 | async-start | bytes 3145728 | tf_op jit(solution)/shard_map/all_gather | solution.py:24
  10.3 64.9 %all-gather.17.cloned.1.call-start = ((), (), s32[]{:S(2)}) async-start(), calls=%async_computation.3 | async-start | bytes 2621440 | tf_op jit(solution)/shard_map/all_gather | solution.py:29
  39.3 76.3 %all-gather.19.cloned.1.call-start = ((), (), s32[]{:S(2)}) async-start(), calls=%async_computation.4 | async-start | bytes 1179648 | tf_op jit(solution)/shard_map/all_gather | solution.py:34
  77.9 168.2 %all-gather.21.cloned.1.call-start = ((), (), s32[]{:S(2)}) async-start(), calls=%async_computation.5 | async-start | bytes 4210688 | tf_op jit(solution)/shard_map/all_gather | solution.py:79
  78.5 187.9 %all-gather.11.cloned.1.call-start = ((), (), s32[]{:S(2)}) async-start(), calls=%async_computation | async-start | bytes 1572864 | tf_op jit(solution)/shard_map/all_gather | solution.py:37
  128.1 169.6 %all-gather.13.cloned.1.call-start = ((), (), s32[]{:S(2)}) async-start(), calls=%async_computation.1 | async-start | bytes 12582912 | tf_op jit(solution)/shard_map/all_gather | solution.py:81
  246.1 1.0 copy-start
  246.1 1.8 copy-start.1
Sparse Core Ops, SparseCore 0:
  10.4 25.6 all-gather.14
  39.4 35.7 all-gather.16
  78.1 37.4 all-gather.18
  119.8 126.3 all-gather.20
  248.1 18.3 all-gather.10
  268.4 29.2 all-gather.12

commit v2 on v1

--- a/solution.py
+++ b/solution.py
@@ -12,29 +12,39 @@
 SEQ_AXES = ("z", "x", "c")
 
 
-def exclusive_sum(stack, index):
-    mask = jnp.arange(stack.shape[0]) < index
-    mask = mask.reshape((-1,) + (1,) * (stack.ndim - 1))
-    return jnp.sum(jnp.where(mask, stack, 0.0), axis=0)
+def exclusive_cumsum(stack):
+    running = jnp.cumsum(stack, axis=0)
+    return jnp.concatenate([jnp.zeros_like(stack[:1]), running[:-1]], axis=0), running[-1]
+
+
+def swap_cores(x):
+    return lax.ppermute(x, "c", [(0, 1), (1, 0)])
 
 
 def prefix_of(own):
-    zi, xi, ci = (lax.axis_index(a) for a in SEQ_AXES)
-    nx, nc = lax.axis_size("x"), lax.axis_size("c")
-    on_chip = lax.all_gather(own, "c")
-    chip_total = jnp.sum(on_chip, axis=0)
-    within_chip = exclusive_sum(on_chip, ci)
+    xi, ci = lax.axis_index("x"), lax.axis_index("c")
+    nz, nx, nc = (lax.axis_size(a) for a in SEQ_AXES)
+    assert nc == 2
+    partner = swap_cores(own)
+    chip_total = own + partner
+    within_chip = jnp.where(ci == 1, partner, jnp.zeros_like(partner))
     half = HEADS // nc
+    quarter = half // nx
     mine = lax.dynamic_slice_in_dim(chip_total, ci * half, half, 0)
-    row = lax.all_gather(mine, "x")
-    before_in_row = exclusive_sum(row, xi)
-    row_total = jnp.sum(row, axis=0)
-    quarter = half // nx
-    piece = lax.dynamic_slice_in_dim(row_total, xi * quarter, quarter, 0)
-    rows = lax.all_gather(piece, "z")
-    before_rows = exclusive_sum(rows, zi)
-    before_rows = lax.all_gather(before_rows, "x", axis=0, tiled=True)
-    chip_prefix = lax.all_gather(before_rows + before_in_row, "c", axis=0, tiled=True)
+    by_chip = lax.all_to_all(mine.reshape(nx, quarter, HEAD, HEAD), "x", 0, 0)
+    before_in_row, row_total = exclusive_cumsum(by_chip)
+    pieces = row_total.reshape(nz, quarter * HEAD // nz, HEAD)
+    by_row = lax.all_to_all(pieces, "z", 0, 0)
+    before_rows, _ = exclusive_cumsum(by_row)
+    before_rows = lax.all_to_all(before_rows, "z", 0, 0).reshape(quarter, HEAD, HEAD)
+    back = lax.all_to_all(before_in_row + before_rows[None], "x", 0, 0)
+    mine = back.reshape(half, HEAD, HEAD)
+    theirs = swap_cores(mine)
+    chip_prefix = jnp.where(
+        ci == 0,
+        jnp.concatenate([mine, theirs], axis=0),
+        jnp.concatenate([theirs, mine], axis=0),
+    )
     return chip_prefix + within_chip
 
 
@@ -76,14 +86,16 @@
     normed = jnp.where(valid[:, None, None], normed, 0.0).astype(jnp.bfloat16)
     rows_per, cols_per = out_weight.shape
     ndp = lax.axis_size("dp")
-    gathered = lax.all_gather(out_weight, ("dp", "z", "x"), axis=0)
-    gathered = gathered.reshape(ndp, nz, nx, rows_per, cols_per)
-    weight = lax.all_gather(gathered, "c", axis=0)
+    ci = lax.axis_index("c")
+    wide = lax.all_gather(out_weight, "dp", axis=1, tiled=True)
+    own_rows = lax.all_gather(wide, ("z", "x"), axis=0, tiled=True)
+    other_rows = swap_cores(own_rows)
     normed = normed.reshape(tok, nz, nx, nc, rows_per)
-    result = jnp.einsum(
-        "tzxcr,cdzxrk->tdk", normed, weight, preferred_element_type=jnp.float32
-    )
-    return result.astype(jnp.bfloat16).reshape(tok, ndp * cols_per)[None]
+    normed_own = jnp.take(normed, ci, axis=3).reshape(tok, nz * nx * rows_per)
+    normed_other = jnp.take(normed, 1 - ci, axis=3).reshape(tok, nz * nx * rows_per)
+    result = jnp.dot(normed_own, own_rows, preferred_element_type=jnp.float32)
+    result = result + jnp.dot(normed_other, other_rows, preferred_element_type=jnp.float32)
+    return result.astype(jnp.bfloat16)[None]
 
 
 def solution(mesh, nx=4, ncore=2):

time: 311 us -> 201 us (0.65)
  waiting for transfers between devices: 263 us -> 86.6 us
  blocking collectives: 10.2 us -> 56 us
  starting transfers between devices: 0.21 us -> 29.8 us
  other arithmetic: 6.6 us -> 1.93 us
    all_gather x6 -> x1, waiting for transfers between devices: 262 us -> 78.4 us  [body(): own_rows = lax.all_gather(wide, ('z', 'x'), axis=0, tiled=True)]
    all_to_all x0 -> x3, blocking collectives: none -> 33.2 us  [the longest x1 11.8 us: prefix_of(): by_chip = lax.all_to_all(mine.reshape(nx, quarter, HEAD, HEAD), 'x', 0, 0)]
    ppermute x0 -> x3, starting transfers between devices: none -> 25.8 us  [swap_cores(): return lax.ppermute(x, 'c', [(0, 1), (1, 0)])]
    all_gather x1, blocking collectives: 10.2 us -> 22.8 us  [body(): wide = lax.all_gather(out_weight, 'dp', axis=1, tiled=True)]
    all_to_all x0 -> x1, waiting for transfers between devices: none -> 7.88 us  [prefix_of(): lax.all_to_all(before_rows, 'z', 0, 0).reshape(quarter, HEAD, HEAD)]
    reduce_sum x3 -> x0, other arithmetic: 5.68 us -> none  [exclusive_sum(): return jnp.sum(jnp.where(mask, stack, 0.0), axis=0)]
    all_to_all x0 -> x1, starting transfers between devices: none -> 4 us  [prefix_of(): lax.all_to_all(before_rows, 'z', 0, 0).reshape(quarter, HEAD, HEAD)]
  transfers between devices with their start and end apart: 6 -> 5, of which waited for: 6 -> 3; matrix products, arithmetic and copies ran while one was open for 2% -> 5% of each run, Pallas kernels for 0% -> 0%
where the time goes in v2:
time: 201 us
  waiting for transfers between devices  86.6 us (43%)
  blocking collectives  56 us (28%)
  starting transfers between devices  29.8 us (15%)
  between operations  14.3 us (7%)
  matrix products  8.46 us (4%)
  local copies, waits for them, and re-layouts  3.4 us (2%)
    all_gather x1, waiting for transfers between devices, body(): own_rows = lax.all_gather(wide, ('z', 'x'), axis=0, tiled=True)  78.4 us
    ppermute x3, starting transfers between devices, swap_cores(): return lax.ppermute(x, 'c', [(0, 1), (1, 0)])  25.8 us
    all_gather x1, blocking collectives, body(): wide = lax.all_gather(out_weight, 'dp', axis=1, tiled=True)  22.8 us
    all_to_all x1, blocking collectives, prefix_of(): by_chip = lax.all_to_all(mine.reshape(nx, quarter, HEAD, HEAD), 'x', 0, 0)  11.8 us
    all_to_all x1, blocking collectives, prefix_of(): by_row = lax.all_to_all(pieces, 'z', 0, 0)  11.4 us
    all_to_all x1, blocking collectives, prefix_of(): back = lax.all_to_all(before_in_row + before_rows[None], 'x', 0, 0)  10 us
    all_to_all x1, waiting for transfers between devices, prefix_of(): lax.all_to_all(before_rows, 'z', 0, 0).reshape(quarter, HEAD, HEAD)  7.88 us
  transfers between devices with their start and end apart: 5, of which 3 were waited for; matrix products, arithmetic and copies ran while one was open for 5% of the time, Pallas kernels for 0%

profile of v2, /device:TPU:1, one launch (start us, length us, event | category | flops | bytes accessed | tf_op | source)
XLA Modules:
  0.0 200.5 jit_solution(4280957788113282783)
XLA Ops:
  6.5 0.0 all-gather.2.cloned.1.call-start
  6.5 22.8 %all_gather.6 = bf16[32,2048]{1,0:T(8,128)(2,1)} all-gather(bf16[32,256]{1,0:T(8,128)(2,1)} %param.13), channel_id=1, replica_groups=mesh['dp'=8,'z'=8,'x'=4,'c'=2] {'dp'}, dimensions={1}, use_global_device_ids=true | all-gather | bytes 147456 | tf_op jit(solution)/shard_map/all_gather | solution.py:90
  29.4 0.0 all-gather.2.cloned.1.call-update
  29.4 1.3 copy.13
  30.7 1.1 copy.15
  31.9 0.3 fusion.21
  32.2 0.0 copy-start.3
  32.2 12.7 %collective-permute-start = (f32[16,128,128]{2,1,0:T(8,128)S(1)}, f32[16,128,128]{2,1,0:T(8,128)S(1)}, u32[]{:S(2)}, u32[]{:S(2)}) collective-permute-start(f32[16,128,128]{2,1,0:T(8,128)S(1)} %fusion.21), channel_id=1, source_target_pairs={{0,1},{1,0},{2,3},{3,2},{4,5},{5,4},{6,7},{7,6},{8,9},{9,8},{10,11... | collective-permute-start | bytes 3145736 | tf_op jit(solution)/shard_map/ppermute | solution.py:21
  44.9 78.4 %all-gather.2.cloned.1.call-done = bf16[1024,2048]{1,0:T(8,128)(2,1)} async-done(((bf16[32,2048]{1,0:T(8,128)(2,1)}), bf16[1024,2048]{1,0:T(8,128)(2,1)}) %all-gather.2.cloned.1.call-update) | async-done | bytes 4194320 | tf_op jit(solution)/shard_map/all_gather | solution.py:91
  123.3 6.3 %collective-permute-start.2 = (bf16[1024,2048]{1,0:T(8,128)(2,1)}, bf16[1024,2048]{1,0:T(8,128)(2,1)}, u32[]{:S(2)}, u32[]{:S(2)}) collective-permute-start(bf16[1024,2048]{1,0:T(8,128)(2,1)} %all-gather.2.cloned.1.call-done), channel_id=1, source_target_pairs={{0,1},{1,0},{2,3},{3,2},{4,5},{5,4},{6,7},{7,6},{8,9},{9,8},{10,11... | collective-permute-start | bytes 12582920 | tf_op jit(solution)/shard_map/ppermute | solution.py:21
  129.6 0.0 collective-permute-done
  129.6 0.0 copy-start.1
  129.6 0.1 dynamic-slice_add_fusion
  129.7 0.0 copy-start.2
  129.7 11.8 %all_to_all.20 = f32[4,2,128,128]{3,2,1,0:T(8,128)S(1)} all-to-all(f32[4,2,128,128]{3,2,1,0:T(8,128)S(1)} %bitcast.47), channel_id=1, replica_groups=mesh['dp'=8,'z'=8,'x'=4,'c'=2] {'x'}, dimensions={0} | all-to-all | bytes 1048576 | tf_op jit(solution)/shard_map/all_to_all | solution.py:34
  141.4 0.3 fusion.26
  141.7 11.4 %all_to_all.21 = f32[8,32,128]{2,1,0:T(8,128)S(1)} all-to-all(f32[8,32,128]{2,1,0:T(8,128)S(1)} %bitcast.52), channel_id=1, replica_groups=mesh['dp'=8,'z'=8,'x'=4,'c'=2] {'z'}, dimensions={0} | all-to-all | bytes 262144 | tf_op jit(solution)/shard_map/all_to_all | solution.py:37
  153.2 0.2 fusion.27
  153.4 0.7 concatenate.13
  154.1 4.0 %all-to-all-start.2 = ((f32[8,32,128]{2,1,0:T(8,128)}), f32[8,32,128]{2,1,0:T(8,128)}, u32[]{:S(2)}, u32[]{:S(2)}) async-start(f32[8,32,128]{2,1,0:T(8,128)} %concatenate.13), calls=%async_computation.2 | async-start | bytes 262144 | tf_op jit(solution)/shard_map/all_to_all | solution.py:39
  158.1 7.9 %all-to-all-done.2 = f32[8,32,128]{2,1,0:T(8,128)} async-done(((f32[8,32,128]{2,1,0:T(8,128)}), f32[8,32,128]{2,1,0:T(8,128)}, u32[]{:S(2)}, u32[]{:S(2)}) %all-to-all-start.2) | async-done | bytes 131104 | tf_op jit(solution)/shard_map/all_to_all | solution.py:39
  166.0 0.9 pad_add_fusion
  167.0 10.0 %all_to_all.22 = f32[4,2,128,128]{3,2,1,0:T(8,128)} all-to-all(f32[4,2,128,128]{3,2,1,0:T(8,128)S(1)} %pad_add_fusion), channel_id=1, replica_groups=mesh['dp'=8,'z'=8,'x'=4,'c'=2] {'x'}, dimensions={0} | all-to-all | bytes 1048576 | tf_op jit(solution)/shard_map/all_to_all | solution.py:40
  177.0 6.8 %collective-permute-start.1 = (f32[8,128,128]{2,1,0:T(8,128)}, f32[8,128,128]{2,1,0:T(8,128)}, u32[]{:S(2)}, u32[]{:S(2)}) collective-permute-start(f32[8,128,128]{2,1,0:T(8,128)} %bitcast.6), channel_id=1, source_target_pairs={{0,1},{1,0},{2,3},{3,2},{4,5},{5,4},{6,7},{7,6},{8,9},{9,8},{10,11... | collective-permute-start | bytes 1572872 | tf_op jit(solution)/shard_map/ppermute | solution.py:21
  184.5 0.0 copy-done.3
  184.5 0.1 mul.49
  184.6 0.0 copy-done.2
  184.6 0.1 copy.14
  184.7 0.0 copy-done.1
  184.8 0.6 convolution_bitcast_fusion
  185.4 0.0 copy-start
  185.4 0.3 collective-permute-done.1
  185.7 3.1 %fusion.10 = (f32[128,16]{0,1:T(8,128)S(1)}, f32[16,128,128]{2,1,0:T(8,128)S(1)}) fusion(f32[16,128,128]{2,1,0:T(8,128)S(1)} %convolution_bitcast_fusion, bf16[128,16,128]{2,1,0:T(8,128)(2,1)S(1)} %bitcast.45, f32[8,128,128]{2,1,0:T(8,128)} %collective-permute-done.1, f32[8,128,128]{2,1,0:T(8,128)} %bitcast.6, f32[16,128,128]{2,1,0:T(8,128)} %copy-done.1, ...), kind=kOutput, calls=%fused_computation.15 | convolution fusion | flops 404748288 | bytes 4726786 | tf_op jit(solution)/shard_map/nthd,nhde->nthe/dot_general | solution.py:77
  188.8 0.3 select_convert_fusion
  189.1 0.1 dynamic-slice_select_fusion
  189.2 0.0 copy-done
  189.2 0.7 fusion.28
  189.9 0.0 collective-permute-done.2
  190.0 3.7 %fusion.1 = bf16[1,128,2048]{2,1,0:T(8,128)(2,1)} fusion(f32[128,2048]{1,0:T(8,128)S(1)} %fusion.28, bf16[128,1024]{0,1:T(8,128)(2,1)S(1)} %bitcast.48, bf16[1024,2048]{1,0:T(8,128)(2,1)} %collective-permute-done.2), kind=kOutput, calls=%fused_computation.2 | convolution fusion | flops 537395200 | bytes 6029312 | tf_op jit(solution)/shard_map/dot_general | solution.py:97
  (7 shorter events, 0.1 us)
Async XLA Ops:
  6.5 116.8 %all-gather.2.cloned.1.call-start = ((), (), s32[]{:S(2)}) async-start(), calls=%async_computation.4 | async-start | bytes 4325376 | tf_op jit(solution)/shard_map/all_gather | solution.py:91
  32.2 152.3 %copy-start.3 = (f32[2048]{0:T(1024)S(1)}, f32[2048]{0:T(1024)}, u32[]{:S(2)}) copy-start(f32[2048]{0:T(1024)} %param.12) | copy-start | bytes 24580
  32.2 97.4 %collective-permute-start = (f32[16,128,128]{2,1,0:T(8,128)S(1)}, f32[16,128,128]{2,1,0:T(8,128)S(1)}, u32[]{:S(2)}, u32[]{:S(2)}) collective-permute-start(f32[16,128,128]{2,1,0:T(8,128)S(1)} %fusion.21), channel_id=1, source_target_pairs={{0,1},{1,0},{2,3},{3,2},{4,5},{5,4},{6,7},{7,6},{8,9},{9,8},{10,11... | collective-permute-start | bytes 3145736 | tf_op jit(solution)/shard_map/ppermute | solution.py:21
  123.3 66.6 %collective-permute-start.2 = (bf16[1024,2048]{1,0:T(8,128)(2,1)}, bf16[1024,2048]{1,0:T(8,128)(2,1)}, u32[]{:S(2)}, u32[]{:S(2)}) collective-permute-start(bf16[1024,2048]{1,0:T(8,128)(2,1)} %all-gather.2.cloned.1.call-done), channel_id=1, source_target_pairs={{0,1},{1,0},{2,3},{3,2},{4,5},{5,4},{6,7},{7,6},{8,9},{9,8},{10,11... | collective-permute-start | bytes 12582920 | tf_op jit(solution)/shard_map/ppermute | solution.py:21
  129.6 55.1 %copy-start.1 = (f32[16,128,128]{2,1,0:T(8,128)}, f32[16,128,128]{2,1,0:T(8,128)S(1)}, u32[]{:S(2)}) copy-start(f32[16,128,128]{2,1,0:T(8,128)S(1)} %collective-permute-done) | copy-start | bytes 3145732
  129.7 54.9 %copy-start.2 = (bf16[1,128,2048]{2,1,0:T(8,128)(2,1)S(1)}, bf16[1,128,2048]{2,1,0:T(8,128)(2,1)}, u32[]{:S(2)}) copy-start(bf16[1,128,2048]{2,1,0:T(8,128)(2,1)} %param.8) | copy-start | bytes 1572868
  154.1 11.9 %all-to-all-start.2 = ((f32[8,32,128]{2,1,0:T(8,128)}), f32[8,32,128]{2,1,0:T(8,128)}, u32[]{:S(2)}, u32[]{:S(2)}) async-start(f32[8,32,128]{2,1,0:T(8,128)} %concatenate.13), calls=%async_computation.2 | async-start | bytes 262144 | tf_op jit(solution)/shard_map/all_to_all | solution.py:39
  177.0 8.7 %collective-permute-start.1 = (f32[8,128,128]{2,1,0:T(8,128)}, f32[8,128,128]{2,1,0:T(8,128)}, u32[]{:S(2)}, u32[]{:S(2)}) collective-permute-start(f32[8,128,128]{2,1,0:T(8,128)} %bitcast.6), channel_id=1, source_target_pairs={{0,1},{1,0},{2,3},{3,2},{4,5},{5,4},{6,7},{7,6},{8,9},{9,8},{10,11... | collective-permute-start | bytes 1572872 | tf_op jit(solution)/shard_map/ppermute | solution.py:21
  185.4 3.8 %copy-start = (bf16[1024,2048]{1,0:T(8,128)(2,1)S(1)}, bf16[1024,2048]{1,0:T(8,128)(2,1)}, u32[]{:S(2)}) copy-start(bf16[1024,2048]{1,0:T(8,128)(2,1)} %all-gather.2.cloned.1.call-done) | copy-start | bytes 12582916
Sparse Core Ops, SparseCore 0:
  29.5 93.7 all-gather.1

commit v3 on v2

--- a/solution.py
+++ b/solution.py
@@ -21,6 +21,33 @@
     return lax.ppermute(x, "c", [(0, 1), (1, 0)])
 
 
+def exchange(x, axis):
+    n, i = lax.axis_size(axis), lax.axis_index(axis)
+    by_offset = [jnp.take(x, i, axis=0)]
+    for s in range(1, n):
+        sent = jnp.take(x, (i + s) % n, axis=0)
+        by_offset.append(lax.ppermute(sent, axis, [(j, (j + s) % n) for j in range(n)]))
+    return jnp.take(jnp.stack(by_offset), (i - jnp.arange(n)) % n, axis=0)
+
+
+def ring_gather(x, axis):
+    n, i = lax.axis_size(axis), lax.axis_index(axis)
+    forward = [(j, (j + 1) % n) for j in range(n)]
+    backward = [(j, (j - 1) % n) for j in range(n)]
+    n_left, n_right = n // 2, (n - 1) // 2
+    from_left, from_right = [], []
+    left = right = x
+    for step in range(max(n_left, n_right)):
+        if step < n_left:
+            left = lax.ppermute(left, axis, forward)
+            from_left.append(left)
+        if step < n_right:
+            right = lax.ppermute(right, axis, backward)
+            from_right.append(right)
+    by_offset = [x] + from_right + from_left[::-1]
+    return jnp.take(jnp.stack(by_offset), (jnp.arange(n) - i) % n, axis=0)
+
+
 def prefix_of(own):
     xi, ci = lax.axis_index("x"), lax.axis_index("c")
     nz, nx, nc = (lax.axis_size(a) for a in SEQ_AXES)
@@ -31,13 +58,13 @@
     half = HEADS // nc
     quarter = half // nx
     mine = lax.dynamic_slice_in_dim(chip_total, ci * half, half, 0)
-    by_chip = lax.all_to_all(mine.reshape(nx, quarter, HEAD, HEAD), "x", 0, 0)
+    by_chip = exchange(mine.reshape(nx, quarter, HEAD, HEAD), "x")
     before_in_row, row_total = exclusive_cumsum(by_chip)
     pieces = row_total.reshape(nz, quarter * HEAD // nz, HEAD)
-    by_row = lax.all_to_all(pieces, "z", 0, 0)
+    by_row = exchange(pieces, "z")
     before_rows, _ = exclusive_cumsum(by_row)
-    before_rows = lax.all_to_all(before_rows, "z", 0, 0).reshape(quarter, HEAD, HEAD)
-    back = lax.all_to_all(before_in_row + before_rows[None], "x", 0, 0)
+    before_rows = exchange(before_rows, "z").reshape(quarter, HEAD, HEAD)
+    back = exchange(before_in_row + before_rows[None], "x")
     mine = back.reshape(half, HEAD, HEAD)
     theirs = swap_cores(mine)
     chip_prefix = jnp.where(
@@ -87,15 +114,25 @@
     rows_per, cols_per = out_weight.shape
     ndp = lax.axis_size("dp")
     ci = lax.axis_index("c")
-    wide = lax.all_gather(out_weight, "dp", axis=1, tiled=True)
-    own_rows = lax.all_gather(wide, ("z", "x"), axis=0, tiled=True)
-    other_rows = swap_cores(own_rows)
+    split = cols_per // 2
+    first = ring_gather(ring_gather(ring_gather(out_weight[:, :split], "dp"), "x"), "z")
+    second = ring_gather(ring_gather(ring_gather(out_weight[:, split:], "z"), "x"), "dp")
+    first_other = swap_cores(first)
+    second_other = swap_cores(second)
     normed = normed.reshape(tok, nz, nx, nc, rows_per)
-    normed_own = jnp.take(normed, ci, axis=3).reshape(tok, nz * nx * rows_per)
-    normed_other = jnp.take(normed, 1 - ci, axis=3).reshape(tok, nz * nx * rows_per)
-    result = jnp.dot(normed_own, own_rows, preferred_element_type=jnp.float32)
-    result = result + jnp.dot(normed_other, other_rows, preferred_element_type=jnp.float32)
-    return result.astype(jnp.bfloat16)[None]
+    normed_own = jnp.take(normed, ci, axis=3)
+    normed_other = jnp.take(normed, 1 - ci, axis=3)
+    f32 = jnp.float32
+    out_first = jnp.einsum("tzxr,zxdrk->tdk", normed_own, first, preferred_element_type=f32)
+    out_first = out_first + jnp.einsum(
+        "tzxr,zxdrk->tdk", normed_other, first_other, preferred_element_type=f32
+    )
+    out_second = jnp.einsum("tzxr,dxzrk->tdk", normed_own, second, preferred_element_type=f32)
+    out_second = out_second + jnp.einsum(
+        "tzxr,dxzrk->tdk", normed_other, second_other, preferred_element_type=f32
+    )
+    result = jnp.concatenate([out_first, out_second], axis=2)
+    return result.astype(jnp.bfloat16).reshape(tok, ndp * cols_per)[None]
 
 
 def solution(mesh, nx=4, ncore=2):

time: 201 us -> 312 us (1.55)
  starting transfers between devices: 29.8 us -> 198 us
  waiting for transfers between devices: 86.6 us -> 27.2 us
  blocking collectives: 56 us -> 0 us
  local copies, waits for them, and re-layouts: 3.4 us -> 45.8 us
  other arithmetic: 1.93 us -> 19.9 us
  between operations: 14.3 us -> 1.99 us
  matrix products: 8.46 us -> 16 us
    ppermute x0 -> x54, starting transfers between devices: none -> 170 us  [the longest x14 70.4 us: ring_gather(): right = lax.ppermute(right, axis, backward)]
    all_gather x1 -> x0, waiting for transfers between devices: 78.4 us -> none  [body(): own_rows = lax.all_gather(wide, ('z', 'x'), axis=0, tiled=True)]
    all_to_all x3 -> x0, blocking collectives: 33.2 us -> none  [the longest x1 11.8 us: prefix_of(): by_chip = lax.all_to_all(mine.reshape(nx, quarter, HEAD, HEAD), 'x', 0, 0)]
    ppermute x0 -> x54, waiting for transfers between devices: none -> 27.2 us  [the longest x20 21.8 us: exchange(): lax.ppermute(sent, axis, [(j, (j + s) % n) for j in range(n)])]
    all_gather x1 -> x0, blocking collectives: 22.8 us -> none  [body(): wide = lax.all_gather(out_weight, 'dp', axis=1, tiled=True)]
    unnamed x10 -> x69, local copies, waits for them, and re-layouts: 1.28 us -> 21.7 us
    gather x0 -> x10, local copies, waits for them, and re-layouts: none -> 18 us  [the longest x4 9.06 us: exchange(): return jnp.take(jnp.stack(by_offset), (i - jnp.arange(n)) % n, axis=0)]
    select_n x1 -> x16, other arithmetic: 0.06 us -> 10.4 us  [the longest x7 5.31 us: ring_gather(): return jnp.take(jnp.stack(by_offset), (jnp.arange(n) - i) % n, axis=0)]
  transfers between devices with their start and end apart: 5 -> 58, of which waited for: 3 -> 8; matrix products, arithmetic and copies ran while one was open for 5% -> 24% of each run, Pallas kernels for 0% -> 0%
where the time goes in v3:
time: 312 us; the launch traced here: 309 us
  starting transfers between devices  198 us (63%)
  local copies, waits for them, and re-layouts  45.8 us (15%)
  waiting for transfers between devices  27.2 us (9%)
  other arithmetic  19.9 us (6%)
  matrix products  16 us (5%)
    ppermute x14, starting transfers between devices, ring_gather(): right = lax.ppermute(right, axis, backward)  70.4 us
    ppermute x20, starting transfers between devices, exchange(): lax.ppermute(sent, axis, [(j, (j + s) % n) for j in range(n)])  59.4 us
    ppermute x20, starting transfers between devices, ring_gather(): left = lax.ppermute(left, axis, forward)  40 us
    ppermute x4, starting transfers between devices, swap_cores(): return lax.ppermute(x, 'c', [(0, 1), (1, 0)])  28.4 us
    ppermute x20, waiting for transfers between devices, exchange(): lax.ppermute(sent, axis, [(j, (j + s) % n) for j in range(n)])  21.8 us
    unnamed x69, local copies, waits for them, and re-layouts  21.7 us
    gather x4, local copies, waits for them, and re-layouts, exchange(): return jnp.take(jnp.stack(by_offset), (i - jnp.arange(n)) % n, axis=0)  9.06 us
    gather x6, local copies, waits for them, and re-layouts, ring_gather(): return jnp.take(jnp.stack(by_offset), (jnp.arange(n) - i) % n, axis=0)  8.9 us
  transfers between devices with their start and end apart: 58, of which 8 were waited for; matrix products, arithmetic and copies ran while one was open for 24% of the time, Pallas kernels for 0%

profile of v3, /device:TPU:1, one launch (start us, length us, event | category | flops | bytes accessed | tf_op | source)
XLA Modules:
  0.0 309.1 jit_solution(11087244112061658891)
XLA Ops:
  0.7 5.9 %collective-permute-start.22 = (bf16[32,128]{1,0:T(8,128)(2,1)S(1)}, bf16[32,128]{1,0:T(8,128)(2,1)S(1)}, u32[]{:S(2)}, u32[]{:S(2)}) collective-permute-start(bf16[32,128]{1,0:T(8,128)(2,1)S(1)} %get-tuple-element.74), channel_id=1, source_target_pairs={{0,448},{64,0},{128,64},{192,128},{256,192},{320,256},{384,320},{4... | collective-permute-start | bytes 24584 | tf_op jit(solution)/shard_map/ppermute | solution.py:45
  8.6 10.7 %collective-permute-start.40 = (bf16[32,128]{1,0:T(8,128)(2,1)S(1)}, bf16[32,128]{1,0:T(8,128)(2,1)S(1)}, u32[]{:S(2)}, u32[]{:S(2)}) collective-permute-start(bf16[32,128]{1,0:T(8,128)(2,1)S(1)} %get-tuple-element.75), channel_id=1, source_target_pairs={{0,56},{8,0},{16,8},{24,16},{32,24},{40,32},{48,40},{56,48},{1,57}... | collective-permute-start | bytes 24584 | tf_op jit(solution)/shard_map/ppermute | solution.py:45
  25.0 3.1 %collective-permute-start = (f32[16,128,128]{2,1,0:T(8,128)}, f32[16,128,128]{2,1,0:T(8,128)}, u32[]{:S(2)}, u32[]{:S(2)}) collective-permute-start(f32[16,128,128]{2,1,0:T(8,128)} %fusion.28), channel_id=1, source_target_pairs={{0,1},{1,0},{2,3},{3,2},{4,5},{5,4},{6,7},{7,6},{8,9},{9,8},{10,11... | collective-permute-start | bytes 3145736 | tf_op jit(solution)/shard_map/ppermute | solution.py:21
  28.4 4.9 %collective-permute-start.23 = (bf16[32,128]{1,0:T(8,128)(2,1)S(1)}, bf16[32,128]{1,0:T(8,128)(2,1)S(1)}, u32[]{:S(2)}, u32[]{:S(2)}) collective-permute-start(bf16[32,128]{1,0:T(8,128)(2,1)S(1)} %collective-permute-done.22), channel_id=1, source_target_pairs={{0,448},{64,0},{128,64},{192,128},{256,192},{320,256},{384,320},{4... | collective-permute-start | bytes 24584 | tf_op jit(solution)/shard_map/ppermute | solution.py:45
  35.2 4.9 %collective-permute-start.41 = (bf16[32,128]{1,0:T(8,128)(2,1)S(1)}, bf16[32,128]{1,0:T(8,128)(2,1)S(1)}, u32[]{:S(2)}, u32[]{:S(2)}) collective-permute-start(bf16[32,128]{1,0:T(8,128)(2,1)S(1)} %collective-permute-done.40), channel_id=1, source_target_pairs={{0,56},{8,0},{16,8},{24,16},{32,24},{40,32},{48,40},{56,48},{1,57}... | collective-permute-start | bytes 24584 | tf_op jit(solution)/shard_map/ppermute | solution.py:45
  42.0 4.6 %collective-permute-start.24 = (bf16[32,128]{1,0:T(8,128)(2,1)S(1)}, bf16[32,128]{1,0:T(8,128)(2,1)S(1)}, u32[]{:S(2)}, u32[]{:S(2)}) collective-permute-start(bf16[32,128]{1,0:T(8,128)(2,1)S(1)} %collective-permute-done.23), channel_id=1, source_target_pairs={{0,448},{64,0},{128,64},{192,128},{256,192},{320,256},{384,320},{4... | collective-permute-start | bytes 24584 | tf_op jit(solution)/shard_map/ppermute | solution.py:45
  48.5 4.6 %collective-permute-start.42 = (bf16[32,128]{1,0:T(8,128)(2,1)S(1)}, bf16[32,128]{1,0:T(8,128)(2,1)S(1)}, u32[]{:S(2)}, u32[]{:S(2)}) collective-permute-start(bf16[32,128]{1,0:T(8,128)(2,1)S(1)} %collective-permute-done.41), channel_id=1, source_target_pairs={{0,56},{8,0},{16,8},{24,16},{32,24},{40,32},{48,40},{56,48},{1,57}... | collective-permute-start | bytes 24584 | tf_op jit(solution)/shard_map/ppermute | solution.py:45
  61.4 3.1 %collective-permute-start.30 = (bf16[8,32,128]{2,1,0:T(8,128)(2,1)S(1)}, bf16[8,32,128]{2,1,0:T(8,128)(2,1)S(1)}, u32[]{:S(2)}, u32[]{:S(2)}) collective-permute-start(bf16[8,32,128]{2,1,0:T(8,128)(2,1)S(1)} %broadcast_select_fusion.6), channel_id=1, source_target_pairs={{0,2},{2,4},{4,6},{6,0},{1,3},{3,5},{5,7},{7,1},{8,10},{10,12},{12... | collective-permute-start | bytes 196616 | tf_op jit(solution)/shard_map/ppermute | solution.py:42
  65.3 4.2 %collective-permute-start.29 = (bf16[8,32,128]{2,1,0:T(8,128)(2,1)S(1)}, bf16[8,32,128]{2,1,0:T(8,128)(2,1)S(1)}, u32[]{:S(2)}, u32[]{:S(2)}) collective-permute-start(bf16[8,32,128]{2,1,0:T(8,128)(2,1)S(1)} %broadcast_select_fusion.6), channel_id=1, source_target_pairs={{0,6},{2,0},{4,2},{6,4},{1,7},{3,1},{5,3},{7,5},{8,14},{10,8},{12,... | collective-permute-start | bytes 196616 | tf_op jit(solution)/shard_map/ppermute | solution.py:45
  71.4 2.3 collective-permute-start.31
  73.8 4.2 %collective-permute-start.47 = (bf16[8,32,128]{2,1,0:T(8,128)(2,1)S(1)}, bf16[8,32,128]{2,1,0:T(8,128)(2,1)S(1)}, u32[]{:S(2)}, u32[]{:S(2)}) collective-permute-start(bf16[8,32,128]{2,1,0:T(8,128)(2,1)S(1)} %broadcast_select_fusion.5), channel_id=1, source_target_pairs={{0,6},{2,0},{4,2},{6,4},{1,7},{3,1},{5,3},{7,5},{8,14},{10,8},{12,... | collective-permute-start | bytes 196616 | tf_op jit(solution)/shard_map/ppermute | solution.py:45
  80.6 3.6 %collective-permute-done.49 = bf16[8,32,128]{2,1,0:T(8,128)(2,1)S(1)} collective-permute-done((bf16[8,32,128]{2,1,0:T(8,128)(2,1)S(1)}, bf16[8,32,128]{2,1,0:T(8,128)(2,1)S(1)}, u32[]{:S(2)}, u32[]{:S(2)}) %collective-permute-start.49) | collective-permute-done | bytes 65568 | tf_op jit(solution)/shard_map/ppermute | solution.py:42
  87.6 3.8 %collective-permute-start.32 = (bf16[4,8,32,128]{3,2,1,0:T(8,128)(2,1)}, bf16[4,8,32,128]{3,2,1,0:T(8,128)(2,1)}, u32[]{:S(2)}, u32[]{:S(2)}) collective-permute-start(bf16[4,8,32,128]{3,2,1,0:T(8,128)(2,1)} %get-tuple-element.47), channel_id=1, source_target_pairs={{0,56},{8,0},{16,8},{24,16},{32,24},{40,32},{48,40},{56,48},{1,57}... | collective-permute-start | bytes 786440 | tf_op jit(solution)/shard_map/ppermute | solution.py:45
  95.2 4.6 %collective-permute-start.50 = (bf16[4,8,32,128]{3,2,1,0:T(8,128)(2,1)}, bf16[4,8,32,128]{3,2,1,0:T(8,128)(2,1)}, u32[]{:S(2)}, u32[]{:S(2)}) collective-permute-start(bf16[4,8,32,128]{3,2,1,0:T(8,128)(2,1)} %get-tuple-element.79), channel_id=1, source_target_pairs={{0,448},{64,0},{128,64},{192,128},{256,192},{320,256},{384,320},{4... | collective-permute-start | bytes 786440 | tf_op jit(solution)/shard_map/ppermute | solution.py:45
  100.4 4.6 %collective-permute-start.33 = (bf16[4,8,32,128]{3,2,1,0:T(8,128)(2,1)}, bf16[4,8,32,128]{3,2,1,0:T(8,128)(2,1)S(1)}, u32[]{:S(2)}, u32[]{:S(2)}) collective-permute-start(bf16[4,8,32,128]{3,2,1,0:T(8,128)(2,1)} %collective-permute-done.32), channel_id=1, source_target_pairs={{0,56},{8,0},{16,8},{24,16},{32,24},{40,32},{48,40},{56,48},{1,57}... | collective-permute-start | bytes 786440 | tf_op jit(solution)/shard_map/ppermute | solution.py:45
  110.6 4.6 %collective-permute-start.51 = (bf16[4,8,32,128]{3,2,1,0:T(8,128)(2,1)}, bf16[4,8,32,128]{3,2,1,0:T(8,128)(2,1)}, u32[]{:S(2)}, u32[]{:S(2)}) collective-permute-start(bf16[4,8,32,128]{3,2,1,0:T(8,128)(2,1)} %collective-permute-done.50), channel_id=1, source_target_pairs={{0,448},{64,0},{128,64},{192,128},{256,192},{320,256},{384,320},{4... | collective-permute-start | bytes 786440 | tf_op jit(solution)/shard_map/ppermute | solution.py:45
  116.2 4.6 %collective-permute-start.34 = (bf16[4,8,32,128]{3,2,1,0:T(8,128)(2,1)S(1)}, bf16[4,8,32,128]{3,2,1,0:T(8,128)(2,1)S(1)}, u32[]{:S(2)}, u32[]{:S(2)}) collective-permute-start(bf16[4,8,32,128]{3,2,1,0:T(8,128)(2,1)S(1)} %collective-permute-done.33), channel_id=1, source_target_pairs={{0,56},{8,0},{16,8},{24,16},{32,24},{40,32},{48,40},{56,48},{1,57}... | collective-permute-start | bytes 786440 | tf_op jit(solution)/shard_map/ppermute | solution.py:45
  127.7 2.2 collective-permute-start.3
  129.9 2.2 collective-permute-start.2
  132.2 2.8 collective-permute-start.1
  135.7 4.6 %collective-permute-start.52 = (bf16[4,8,32,128]{3,2,1,0:T(8,128)(2,1)}, bf16[4,8,32,128]{3,2,1,0:T(8,128)(2,1)S(1)}, u32[]{:S(2)}, u32[]{:S(2)}) collective-permute-start(bf16[4,8,32,128]{3,2,1,0:T(8,128)(2,1)} %collective-permute-done.51), channel_id=1, source_target_pairs={{0,448},{64,0},{128,64},{192,128},{256,192},{320,256},{384,320},{4... | collective-permute-start | bytes 786440 | tf_op jit(solution)/shard_map/ppermute | solution.py:45
  145.0 2.4 gather_fusion
  151.3 4.7 %collective-permute-start.10 = (f32[32,128]{1,0:T(8,128)S(1)}, f32[32,128]{1,0:T(8,128)S(1)}, u32[]{:S(2)}, u32[]{:S(2)}) collective-permute-start(f32[32,128]{1,0:T(8,128)S(1)} %get-tuple-element.58), channel_id=1, source_target_pairs={{0,56},{8,0},{16,8},{24,16},{32,24},{40,32},{48,40},{56,48},{1,57}... | collective-permute-start | bytes 49160 | tf_op jit(solution)/shard_map/ppermute | solution.py:29
  156.0 4.5 %collective-permute-start.9 = (f32[32,128]{1,0:T(8,128)S(1)}, f32[32,128]{1,0:T(8,128)S(1)}, u32[]{:S(2)}, u32[]{:S(2)}) collective-permute-start(f32[32,128]{1,0:T(8,128)S(1)} %get-tuple-element.59), channel_id=1, source_target_pairs={{0,48},{8,56},{16,0},{24,8},{32,16},{40,24},{48,32},{56,40},{1,49}... | collective-permute-start | bytes 49160 | tf_op jit(solution)/shard_map/ppermute | solution.py:29
  163.1 4.1 %collective-permute-done.5 = f32[32,128]{1,0:T(8,128)S(1)} collective-permute-done((f32[32,128]{1,0:T(8,128)S(1)}, f32[32,128]{1,0:T(8,128)S(1)}, u32[]{:S(2)}, u32[]{:S(2)}) %collective-permute-start.5) | collective-permute-done | bytes 16416 | tf_op jit(solution)/shard_map/ppermute | solution.py:29
  169.7 5.0 %collective-permute-done.6 = f32[32,128]{1,0:T(8,128)S(1)} collective-permute-done((f32[32,128]{1,0:T(8,128)S(1)}, f32[32,128]{1,0:T(8,128)S(1)}, u32[]{:S(2)}, u32[]{:S(2)}) %collective-permute-start.6) | collective-permute-done | bytes 16416 | tf_op jit(solution)/shard_map/ppermute | solution.py:29
  177.2 5.9 %collective-permute-done.7 = f32[32,128]{1,0:T(8,128)S(1)} collective-permute-done((f32[32,128]{1,0:T(8,128)S(1)}, f32[32,128]{1,0:T(8,128)S(1)}, u32[]{:S(2)}, u32[]{:S(2)}) %collective-permute-start.7) | collective-permute-done | bytes 16416 | tf_op jit(solution)/shard_map/ppermute | solution.py:29
  185.6 3.9 %collective-permute-done.8 = f32[32,128]{1,0:T(8,128)S(1)} collective-permute-done((f32[32,128]{1,0:T(8,128)S(1)}, f32[32,128]{1,0:T(8,128)S(1)}, u32[]{:S(2)}, u32[]{:S(2)}) %collective-permute-start.8) | collective-permute-done | bytes 16416 | tf_op jit(solution)/shard_map/ppermute | solution.py:29
  194.5 2.9 collective-permute-start.11
  198.0 3.6 %collective-permute-start.17 = (f32[32,128]{1,0:T(8,128)S(1)}, f32[32,128]{1,0:T(8,128)S(1)}, u32[]{:S(2)}, u32[]{:S(2)}) collective-permute-start(f32[32,128]{1,0:T(8,128)S(1)} %get-tuple-element.66), channel_id=1, source_target_pairs={{0,56},{8,0},{16,8},{24,16},{32,24},{40,32},{48,40},{56,48},{1,57}... | collective-permute-start | bytes 49160 | tf_op jit(solution)/shard_map/ppermute | solution.py:29
  203.6 2.9 collective-permute-start.13
  208.2 4.9 %collective-permute-start.14 = (f32[32,128]{1,0:T(8,128)S(1)}, f32[32,128]{1,0:T(8,128)S(1)}, u32[]{:S(2)}, u32[]{:S(2)}) collective-permute-start(f32[32,128]{1,0:T(8,128)S(1)} %get-tuple-element.70), channel_id=1, source_target_pairs={{0,32},{8,40},{16,48},{24,56},{32,0},{40,8},{48,16},{56,24},{1,33}... | collective-permute-start | bytes 49160 | tf_op jit(solution)/shard_map/ppermute | solution.py:29
  213.7 3.3 %collective-permute-start.15 = (f32[32,128]{1,0:T(8,128)S(1)}, f32[32,128]{1,0:T(8,128)S(1)}, u32[]{:S(2)}, u32[]{:S(2)}) collective-permute-start(f32[32,128]{1,0:T(8,128)S(1)} %get-tuple-element.71), channel_id=1, source_target_pairs={{0,40},{8,48},{16,56},{24,0},{32,8},{40,16},{48,24},{56,32},{1,41}... | collective-permute-start | bytes 49160 | tf_op jit(solution)/shard_map/ppermute | solution.py:29
  217.6 3.9 %collective-permute-start.16 = (f32[32,128]{1,0:T(8,128)S(1)}, f32[32,128]{1,0:T(8,128)S(1)}, u32[]{:S(2)}, u32[]{:S(2)}) collective-permute-start(f32[32,128]{1,0:T(8,128)S(1)} %get-tuple-element.72), channel_id=1, source_target_pairs={{0,48},{8,56},{16,0},{24,8},{32,16},{40,24},{48,32},{56,40},{1,49}... | collective-permute-start | bytes 49160 | tf_op jit(solution)/shard_map/ppermute | solution.py:29
  229.6 4.3 %collective-permute-start.20 = (f32[2,128,128]{2,1,0:T(8,128)}, f32[2,128,128]{2,1,0:T(8,128)}, u32[]{:S(2)}, u32[]{:S(2)}) collective-permute-start(f32[2,128,128]{2,1,0:T(8,128)} %get-tuple-element.51), channel_id=1, source_target_pairs={{0,6},{2,0},{4,2},{6,4},{1,7},{3,1},{5,3},{7,5},{8,14},{10,8},{12,... | collective-permute-start | bytes 393224 | tf_op jit(solution)/shard_map/ppermute | solution.py:29
  233.9 3.0 collective-permute-start.19
  236.9 2.8 collective-permute-start.18
  242.7 2.1 gather_fusion.9
  246.8 20.7 %collective-permute-start.57 = (bf16[8,4,8,32,128]{4,3,2,1,0:T(8,128)(2,1)S(1)}, bf16[8,4,8,32,128]{4,3,2,1,0:T(8,128)(2,1)}, u32[]{:S(2)}, u32[]{:S(2)}) collective-permute-start(bf16[8,4,8,32,128]{4,3,2,1,0:T(8,128)(2,1)S(1)} %broadcast_select_fusion), channel_id=1, source_target_pairs={{0,1},{1,0},{2,3},{3,2},{4,5},{5,4},{6,7},{7,6},{8,9},{9,8},{10,11... | collective-permute-start | bytes 6291464 | tf_op jit(solution)/shard_map/ppermute | solution.py:21
  272.3 3.8 %gather_fusion.6 = bf16[8,4,8,32,128]{4,3,2,1,0:T(8,128)(2,1)} fusion(bf16[8,4,8,32,128]{4,3,2,1,0:T(8,128)(2,1)} %bitcast_dynamic-update-slice_fusion, s32[1024]{0:T(1024)S(1)} %pad_clamp_fusion), kind=kCustom, calls=%fused_computation.4.clone | custom fusion | bytes 4194336 | tf_op jit(solution)/shard_map/jit(_take)/gather | solution.py:48
  276.1 3.2 %copy_select_fusion = bf16[8,4,8,32,128]{4,3,0,1,2:T(8,128)(2,1)} fusion(bf16[8,4,8,32,128]{4,3,2,1,0:T(8,128)(2,1)} %gather_fusion.6, pred[8]{0:T(512)(128)(4,1)S(1)} %copy-done.10), kind=kLoop, calls=%fused_computation.10 | loop fusion | flops 1048576 | bytes 4194312 | tf_op jit(solution)/shard_map/jit(_take)/select_n | solution.py:48
  283.2 2.4 gather_fusion.3
  287.6 2.6 collective-permute-start.21
  292.9 2.7 convolution_bitcast_fusion
  295.7 3.4 %fusion.12 = (f32[128,16]{0,1:T(8,128)S(1)}, f32[16,128,128]{2,1,0:T(8,128)S(1)}) fusion(f32[16,128,128]{2,1,0:T(8,128)} %convolution_bitcast_fusion, bf16[128,16,128]{2,1,0:T(8,128)(2,1)} %bitcast.244, f32[8,128,128]{2,1,0:T(8,128)} %collective-permute-done.21, f32[8,128,128]{2,1,0:T(8,128)} %bitcast.72, f32[16,128,128]{2,1,0:T(8,128)} %collective-permute-done, ...), kind=kOutput, calls=%fused_computation.32 | convolution fusion | flops 404748288 | bytes 4726786 | tf_op jit(solution)/shard_map/nthd,nhde->nthe/dot_general | solution.py:104
  299.5 2.5 convolution_bitcast_fusion.1
  303.0 2.5 convolution_bitcast_fusion.3
  305.5 2.5 fusion.4
  (212 shorter events, 106.8 us)
Async XLA Ops:
  0.7 27.6 %collective-permute-start.22 = (bf16[32,128]{1,0:T(8,128)(2,1)S(1)}, bf16[32,128]{1,0:T(8,128)(2,1)S(1)}, u32[]{:S(2)}, u32[]{:S(2)}) collective-permute-start(bf16[32,128]{1,0:T(8,128)(2,1)S(1)} %get-tuple-element.74), channel_id=1, source_target_pairs={{0,448},{64,0},{128,64},{192,128},{256,192},{320,256},{384,320},{4... | collective-permute-start | bytes 24584 | tf_op jit(solution)/shard_map/ppermute | solution.py:45
  6.6 26.6 %collective-permute-start.25 = (bf16[32,128]{1,0:T(8,128)(2,1)S(1)}, bf16[32,128]{1,0:T(8,128)(2,1)S(1)}, u32[]{:S(2)}, u32[]{:S(2)}) collective-permute-start(bf16[32,128]{1,0:T(8,128)(2,1)S(1)} %get-tuple-element.74), channel_id=1, source_target_pairs={{0,64},{64,128},{128,192},{192,256},{256,320},{320,384},{384,448},... | collective-permute-start | bytes 24584 | tf_op jit(solution)/shard_map/ppermute | solution.py:42
  8.6 26.6 %collective-permute-start.40 = (bf16[32,128]{1,0:T(8,128)(2,1)S(1)}, bf16[32,128]{1,0:T(8,128)(2,1)S(1)}, u32[]{:S(2)}, u32[]{:S(2)}) collective-permute-start(bf16[32,128]{1,0:T(8,128)(2,1)S(1)} %get-tuple-element.75), channel_id=1, source_target_pairs={{0,56},{8,0},{16,8},{24,16},{32,24},{40,32},{48,40},{56,48},{1,57}... | collective-permute-start | bytes 24584 | tf_op jit(solution)/shard_map/ppermute | solution.py:45
  19.2 20.8 %collective-permute-start.43 = (bf16[32,128]{1,0:T(8,128)(2,1)S(1)}, bf16[32,128]{1,0:T(8,128)(2,1)S(1)}, u32[]{:S(2)}, u32[]{:S(2)}) collective-permute-start(bf16[32,128]{1,0:T(8,128)(2,1)S(1)} %get-tuple-element.75), channel_id=1, source_target_pairs={{0,8},{8,16},{16,24},{24,32},{32,40},{40,48},{48,56},{56,0},{1,9},... | collective-permute-start | bytes 24584 | tf_op jit(solution)/shard_map/ppermute | solution.py:42
  25.0 101.4 %collective-permute-start = (f32[16,128,128]{2,1,0:T(8,128)}, f32[16,128,128]{2,1,0:T(8,128)}, u32[]{:S(2)}, u32[]{:S(2)}) collective-permute-start(f32[16,128,128]{2,1,0:T(8,128)} %fusion.28), channel_id=1, source_target_pairs={{0,1},{1,0},{2,3},{3,2},{4,5},{5,4},{6,7},{7,6},{8,9},{9,8},{10,11... | collective-permute-start | bytes 3145736 | tf_op jit(solution)/shard_map/ppermute | solution.py:21
  28.4 13.6 %collective-permute-start.23 = (bf16[32,128]{1,0:T(8,128)(2,1)S(1)}, bf16[32,128]{1,0:T(8,128)(2,1)S(1)}, u32[]{:S(2)}, u32[]{:S(2)}) collective-permute-start(bf16[32,128]{1,0:T(8,128)(2,1)S(1)} %collective-permute-done.22), channel_id=1, source_target_pairs={{0,448},{64,0},{128,64},{192,128},{256,192},{320,256},{384,320},{4... | collective-permute-start | bytes 24584 | tf_op jit(solution)/shard_map/ppermute | solution.py:45
  33.2 13.4 %collective-permute-start.26 = (bf16[32,128]{1,0:T(8,128)(2,1)S(1)}, bf16[32,128]{1,0:T(8,128)(2,1)S(1)}, u32[]{:S(2)}, u32[]{:S(2)}) collective-permute-start(bf16[32,128]{1,0:T(8,128)(2,1)S(1)} %collective-permute-done.25), channel_id=1, source_target_pairs={{0,64},{64,128},{128,192},{192,256},{256,320},{320,384},{384,448},... | collective-permute-start | bytes 24584 | tf_op jit(solution)/shard_map/ppermute | solution.py:42
  35.2 13.4 %collective-permute-start.41 = (bf16[32,128]{1,0:T(8,128)(2,1)S(1)}, bf16[32,128]{1,0:T(8,128)(2,1)S(1)}, u32[]{:S(2)}, u32[]{:S(2)}) collective-permute-start(bf16[32,128]{1,0:T(8,128)(2,1)S(1)} %collective-permute-done.40), channel_id=1, source_target_pairs={{0,56},{8,0},{16,8},{24,16},{32,24},{40,32},{48,40},{56,48},{1,57}... | collective-permute-start | bytes 24584 | tf_op jit(solution)/shard_map/ppermute | solution.py:45
  40.0 13.1 %collective-permute-start.44 = (bf16[32,128]{1,0:T(8,128)(2,1)S(1)}, bf16[32,128]{1,0:T(8,128)(2,1)S(1)}, u32[]{:S(2)}, u32[]{:S(2)}) collective-permute-start(bf16[32,128]{1,0:T(8,128)(2,1)S(1)} %collective-permute-done.43), channel_id=1, source_target_pairs={{0,8},{8,16},{16,24},{24,32},{32,40},{40,48},{48,56},{56,0},{1,9},... | collective-permute-start | bytes 24584 | tf_op jit(solution)/shard_map/ppermute | solution.py:42
  42.0 18.6 %collective-permute-start.24 = (bf16[32,128]{1,0:T(8,128)(2,1)S(1)}, bf16[32,128]{1,0:T(8,128)(2,1)S(1)}, u32[]{:S(2)}, u32[]{:S(2)}) collective-permute-start(bf16[32,128]{1,0:T(8,128)(2,1)S(1)} %collective-permute-done.23), channel_id=1, source_target_pairs={{0,448},{64,0},{128,64},{192,128},{256,192},{320,256},{384,320},{4... | collective-permute-start | bytes 24584 | tf_op jit(solution)/shard_map/ppermute | solution.py:45
  46.6 8.5 %collective-permute-start.27 = (bf16[32,128]{1,0:T(8,128)(2,1)S(1)}, bf16[32,128]{1,0:T(8,128)(2,1)S(1)}, u32[]{:S(2)}, u32[]{:S(2)}) collective-permute-start(bf16[32,128]{1,0:T(8,128)(2,1)S(1)} %collective-permute-done.26), channel_id=1, source_target_pairs={{0,64},{64,128},{128,192},{192,256},{256,320},{320,384},{384,448},... | collective-permute-start | bytes 24584 | tf_op jit(solution)/shard_map/ppermute | solution.py:42
  48.5 12.1 %collective-permute-start.42 = (bf16[32,128]{1,0:T(8,128)(2,1)S(1)}, bf16[32,128]{1,0:T(8,128)(2,1)S(1)}, u32[]{:S(2)}, u32[]{:S(2)}) collective-permute-start(bf16[32,128]{1,0:T(8,128)(2,1)S(1)} %collective-permute-done.41), channel_id=1, source_target_pairs={{0,56},{8,0},{16,8},{24,16},{32,24},{40,32},{48,40},{56,48},{1,57}... | collective-permute-start | bytes 24584 | tf_op jit(solution)/shard_map/ppermute | solution.py:45
  61.4 10.0 %collective-permute-start.30 = (bf16[8,32,128]{2,1,0:T(8,128)(2,1)S(1)}, bf16[8,32,128]{2,1,0:T(8,128)(2,1)S(1)}, u32[]{:S(2)}, u32[]{:S(2)}) collective-permute-start(bf16[8,32,128]{2,1,0:T(8,128)(2,1)S(1)} %broadcast_select_fusion.6), channel_id=1, source_target_pairs={{0,2},{2,4},{4,6},{6,0},{1,3},{3,5},{5,7},{7,1},{8,10},{10,12},{12... | collective-permute-start | bytes 196616 | tf_op jit(solution)/shard_map/ppermute | solution.py:42
  65.3 14.6 %collective-permute-start.29 = (bf16[8,32,128]{2,1,0:T(8,128)(2,1)S(1)}, bf16[8,32,128]{2,1,0:T(8,128)(2,1)S(1)}, u32[]{:S(2)}, u32[]{:S(2)}) collective-permute-start(bf16[8,32,128]{2,1,0:T(8,128)(2,1)S(1)} %broadcast_select_fusion.6), channel_id=1, source_target_pairs={{0,6},{2,0},{4,2},{6,4},{1,7},{3,1},{5,3},{7,5},{8,14},{10,8},{12,... | collective-permute-start | bytes 196616 | tf_op jit(solution)/shard_map/ppermute | solution.py:45
  69.5 8.5 %collective-permute-start.48 = (bf16[8,32,128]{2,1,0:T(8,128)(2,1)S(1)}, bf16[8,32,128]{2,1,0:T(8,128)(2,1)S(1)}, u32[]{:S(2)}, u32[]{:S(2)}) collective-permute-start(bf16[8,32,128]{2,1,0:T(8,128)(2,1)S(1)} %broadcast_select_fusion.5), channel_id=1, source_target_pairs={{0,2},{2,4},{4,6},{6,0},{1,3},{3,5},{5,7},{7,1},{8,10},{10,12},{12... | collective-permute-start | bytes 196616 | tf_op jit(solution)/shard_map/ppermute | solution.py:42
  71.4 8.5 %collective-permute-start.31 = (bf16[8,32,128]{2,1,0:T(8,128)(2,1)S(1)}, bf16[8,32,128]{2,1,0:T(8,128)(2,1)S(1)}, u32[]{:S(2)}, u32[]{:S(2)}) collective-permute-start(bf16[8,32,128]{2,1,0:T(8,128)(2,1)S(1)} %collective-permute-done.30), channel_id=1, source_target_pairs={{0,2},{2,4},{4,6},{6,0},{1,3},{3,5},{5,7},{7,1},{8,10},{10,12},{12... | collective-permute-start | bytes 196616 | tf_op jit(solution)/shard_map/ppermute | solution.py:42
  87.6 12.9 %collective-permute-start.32 = (bf16[4,8,32,128]{3,2,1,0:T(8,128)(2,1)}, bf16[4,8,32,128]{3,2,1,0:T(8,128)(2,1)}, u32[]{:S(2)}, u32[]{:S(2)}) collective-permute-start(bf16[4,8,32,128]{3,2,1,0:T(8,128)(2,1)} %get-tuple-element.47), channel_id=1, source_target_pairs={{0,56},{8,0},{16,8},{24,16},{32,24},{40,32},{48,40},{56,48},{1,57}... | collective-permute-start | bytes 786440 | tf_op jit(solution)/shard_map/ppermute | solution.py:45
  91.4 13.6 %collective-permute-start.35 = (bf16[4,8,32,128]{3,2,1,0:T(8,128)(2,1)}, bf16[4,8,32,128]{3,2,1,0:T(8,128)(2,1)S(1)}, u32[]{:S(2)}, u32[]{:S(2)}) collective-permute-start(bf16[4,8,32,128]{3,2,1,0:T(8,128)(2,1)} %get-tuple-element.47), channel_id=1, source_target_pairs={{0,8},{8,16},{16,24},{24,32},{32,40},{40,48},{48,56},{56,0},{1,9},... | collective-permute-start | bytes 786440 | tf_op jit(solution)/shard_map/ppermute | solution.py:42
  93.3 13.7 %collective-permute-start.53 = (bf16[4,8,32,128]{3,2,1,0:T(8,128)(2,1)}, bf16[4,8,32,128]{3,2,1,0:T(8,128)(2,1)}, u32[]{:S(2)}, u32[]{:S(2)}) collective-permute-start(bf16[4,8,32,128]{3,2,1,0:T(8,128)(2,1)} %get-tuple-element.79), channel_id=1, source_target_pairs={{0,64},{64,128},{128,192},{192,256},{256,320},{320,384},{384,448},... | collective-permute-start | bytes 786440 | tf_op jit(solution)/shard_map/ppermute | solution.py:42
  95.2 15.3 %collective-permute-start.50 = (bf16[4,8,32,128]{3,2,1,0:T(8,128)(2,1)}, bf16[4,8,32,128]{3,2,1,0:T(8,128)(2,1)}, u32[]{:S(2)}, u32[]{:S(2)}) collective-permute-start(bf16[4,8,32,128]{3,2,1,0:T(8,128)(2,1)} %get-tuple-element.79), channel_id=1, source_target_pairs={{0,448},{64,0},{128,64},{192,128},{256,192},{320,256},{384,320},{4... | collective-permute-start | bytes 786440 | tf_op jit(solution)/shard_map/ppermute | solution.py:45
  100.4 15.7 %collective-permute-start.33 = (bf16[4,8,32,128]{3,2,1,0:T(8,128)(2,1)}, bf16[4,8,32,128]{3,2,1,0:T(8,128)(2,1)S(1)}, u32[]{:S(2)}, u32[]{:S(2)}) collective-permute-start(bf16[4,8,32,128]{3,2,1,0:T(8,128)(2,1)} %collective-permute-done.32), channel_id=1, source_target_pairs={{0,56},{8,0},{16,8},{24,16},{32,24},{40,32},{48,40},{56,48},{1,57}... | collective-permute-start | bytes 786440 | tf_op jit(solution)/shard_map/ppermute | solution.py:45
  105.0 15.7 %collective-permute-start.36 = (bf16[4,8,32,128]{3,2,1,0:T(8,128)(2,1)S(1)}, bf16[4,8,32,128]{3,2,1,0:T(8,128)(2,1)S(1)}, u32[]{:S(2)}, u32[]{:S(2)}) collective-permute-start(bf16[4,8,32,128]{3,2,1,0:T(8,128)(2,1)S(1)} %collective-permute-done.35), channel_id=1, source_target_pairs={{0,8},{8,16},{16,24},{24,32},{32,40},{40,48},{48,56},{56,0},{1,9},... | collective-permute-start | bytes 786440 | tf_op jit(solution)/shard_map/ppermute | solution.py:42
  107.0 15.7 %collective-permute-start.54 = (bf16[4,8,32,128]{3,2,1,0:T(8,128)(2,1)}, bf16[4,8,32,128]{3,2,1,0:T(8,128)(2,1)S(1)}, u32[]{:S(2)}, u32[]{:S(2)}) collective-permute-start(bf16[4,8,32,128]{3,2,1,0:T(8,128)(2,1)} %collective-permute-done.53), channel_id=1, source_target_pairs={{0,64},{64,128},{128,192},{192,256},{256,320},{320,384},{384,448},... | collective-permute-start | bytes 786440 | tf_op jit(solution)/shard_map/ppermute | solution.py:42
  110.6 14.8 %collective-permute-start.51 = (bf16[4,8,32,128]{3,2,1,0:T(8,128)(2,1)}, bf16[4,8,32,128]{3,2,1,0:T(8,128)(2,1)}, u32[]{:S(2)}, u32[]{:S(2)}) collective-permute-start(bf16[4,8,32,128]{3,2,1,0:T(8,128)(2,1)} %collective-permute-done.50), channel_id=1, source_target_pairs={{0,448},{64,0},{128,64},{192,128},{256,192},{320,256},{384,320},{4... | collective-permute-start | bytes 786440 | tf_op jit(solution)/shard_map/ppermute | solution.py:45
  116.2 16.0 %collective-permute-start.34 = (bf16[4,8,32,128]{3,2,1,0:T(8,128)(2,1)S(1)}, bf16[4,8,32,128]{3,2,1,0:T(8,128)(2,1)S(1)}, u32[]{:S(2)}, u32[]{:S(2)}) collective-permute-start(bf16[4,8,32,128]{3,2,1,0:T(8,128)(2,1)S(1)} %collective-permute-done.33), channel_id=1, source_target_pairs={{0,56},{8,0},{16,8},{24,16},{32,24},{40,32},{48,40},{56,48},{1,57}... | collective-permute-start | bytes 786440 | tf_op jit(solution)/shard_map/ppermute | solution.py:45
  120.8 14.9 %collective-permute-start.37 = (bf16[4,8,32,128]{3,2,1,0:T(8,128)(2,1)S(1)}, bf16[4,8,32,128]{3,2,1,0:T(8,128)(2,1)}, u32[]{:S(2)}, u32[]{:S(2)}) collective-permute-start(bf16[4,8,32,128]{3,2,1,0:T(8,128)(2,1)S(1)} %collective-permute-done.36), channel_id=1, source_target_pairs={{0,8},{8,16},{16,24},{24,32},{32,40},{40,48},{48,56},{56,0},{1,9},... | collective-permute-start | bytes 786440 | tf_op jit(solution)/shard_map/ppermute | solution.py:42
  122.7 17.5 %collective-permute-start.55 = (bf16[4,8,32,128]{3,2,1,0:T(8,128)(2,1)S(1)}, bf16[4,8,32,128]{3,2,1,0:T(8,128)(2,1)}, u32[]{:S(2)}, u32[]{:S(2)}) collective-permute-start(bf16[4,8,32,128]{3,2,1,0:T(8,128)(2,1)S(1)} %collective-permute-done.54), channel_id=1, source_target_pairs={{0,64},{64,128},{128,192},{192,256},{256,320},{320,384},{384,448},... | collective-permute-start | bytes 786440 | tf_op jit(solution)/shard_map/ppermute | solution.py:42
  127.7 14.5 %collective-permute-start.3 = (f32[2,128,128]{2,1,0:T(8,128)S(1)}, f32[2,128,128]{2,1,0:T(8,128)S(1)}, u32[]{:S(2)}, u32[]{:S(2)}) collective-permute-start(f32[2,128,128]{2,1,0:T(8,128)S(1)} %get-tuple-element.55), channel_id=1, source_target_pairs={{0,6},{2,0},{4,2},{6,4},{1,7},{3,1},{5,3},{7,5},{8,14},{10,8},{12,... | collective-permute-start | bytes 393224 | tf_op jit(solution)/shard_map/ppermute | solution.py:29
  129.9 14.2 %collective-permute-start.2 = (f32[2,128,128]{2,1,0:T(8,128)S(1)}, f32[2,128,128]{2,1,0:T(8,128)S(1)}, u32[]{:S(2)}, u32[]{:S(2)}) collective-permute-start(f32[2,128,128]{2,1,0:T(8,128)S(1)} %get-tuple-element.56), channel_id=1, source_target_pairs={{0,4},{2,6},{4,0},{6,2},{1,5},{3,7},{5,1},{7,3},{8,12},{10,14},{12... | collective-permute-start | bytes 393224 | tf_op jit(solution)/shard_map/ppermute | solution.py:29
  132.2 12.0 %collective-permute-start.1 = (f32[2,128,128]{2,1,0:T(8,128)S(1)}, f32[2,128,128]{2,1,0:T(8,128)S(1)}, u32[]{:S(2)}, u32[]{:S(2)}) collective-permute-start(f32[2,128,128]{2,1,0:T(8,128)S(1)} %get-tuple-element.57), channel_id=1, source_target_pairs={{0,2},{2,4},{4,6},{6,0},{1,3},{3,5},{5,7},{7,1},{8,10},{10,12},{12... | collective-permute-start | bytes 393224 | tf_op jit(solution)/shard_map/ppermute | solution.py:29
  135.7 15.6 %collective-permute-start.52 = (bf16[4,8,32,128]{3,2,1,0:T(8,128)(2,1)}, bf16[4,8,32,128]{3,2,1,0:T(8,128)(2,1)S(1)}, u32[]{:S(2)}, u32[]{:S(2)}) collective-permute-start(bf16[4,8,32,128]{3,2,1,0:T(8,128)(2,1)} %collective-permute-done.51), channel_id=1, source_target_pairs={{0,448},{64,0},{128,64},{192,128},{256,192},{320,256},{384,320},{4... | collective-permute-start | bytes 786440 | tf_op jit(solution)/shard_map/ppermute | solution.py:45
  140.3 127.2 %collective-permute-start.38 = (bf16[4,8,32,128]{3,2,1,0:T(8,128)(2,1)}, bf16[4,8,32,128]{3,2,1,0:T(8,128)(2,1)}, u32[]{:S(2)}, u32[]{:S(2)}) collective-permute-start(bf16[4,8,32,128]{3,2,1,0:T(8,128)(2,1)} %collective-permute-done.37), channel_id=1, source_target_pairs={{0,8},{8,16},{16,24},{24,32},{32,40},{40,48},{48,56},{56,0},{1,9},... | collective-permute-start | bytes 786440 | tf_op jit(solution)/shard_map/ppermute | solution.py:42
  142.2 97.5 %collective-permute-start.56 = (bf16[4,8,32,128]{3,2,1,0:T(8,128)(2,1)}, bf16[4,8,32,128]{3,2,1,0:T(8,128)(2,1)}, u32[]{:S(2)}, u32[]{:S(2)}) collective-permute-start(bf16[4,8,32,128]{3,2,1,0:T(8,128)(2,1)} %collective-permute-done.55), channel_id=1, source_target_pairs={{0,64},{64,128},{128,192},{192,256},{256,320},{320,384},{384,448},... | collective-permute-start | bytes 786440 | tf_op jit(solution)/shard_map/ppermute | solution.py:42
  149.3 11.2 %collective-permute-start.4 = (f32[32,128]{1,0:T(8,128)S(1)}, f32[32,128]{1,0:T(8,128)S(1)}, u32[]{:S(2)}, u32[]{:S(2)}) collective-permute-start(f32[32,128]{1,0:T(8,128)S(1)} %get-tuple-element.64), channel_id=1, source_target_pairs={{0,8},{8,16},{16,24},{24,32},{32,40},{40,48},{48,56},{56,0},{1,9},... | collective-permute-start | bytes 49160 | tf_op jit(solution)/shard_map/ppermute | solution.py:29
  151.3 39.4 %collective-permute-start.10 = (f32[32,128]{1,0:T(8,128)S(1)}, f32[32,128]{1,0:T(8,128)S(1)}, u32[]{:S(2)}, u32[]{:S(2)}) collective-permute-start(f32[32,128]{1,0:T(8,128)S(1)} %get-tuple-element.58), channel_id=1, source_target_pairs={{0,56},{8,0},{16,8},{24,16},{32,24},{40,32},{48,40},{56,48},{1,57}... | collective-permute-start | bytes 49160 | tf_op jit(solution)/shard_map/ppermute | solution.py:29
  156.0 34.1 %collective-permute-start.9 = (f32[32,128]{1,0:T(8,128)S(1)}, f32[32,128]{1,0:T(8,128)S(1)}, u32[]{:S(2)}, u32[]{:S(2)}) collective-permute-start(f32[32,128]{1,0:T(8,128)S(1)} %get-tuple-element.59), channel_id=1, source_target_pairs={{0,48},{8,56},{16,0},{24,8},{32,16},{40,24},{48,32},{56,40},{1,49}... | collective-permute-start | bytes 49160 | tf_op jit(solution)/shard_map/ppermute | solution.py:29
  174.7 8.5 %collective-permute-start.7 = (f32[32,128]{1,0:T(8,128)S(1)}, f32[32,128]{1,0:T(8,128)S(1)}, u32[]{:S(2)}, u32[]{:S(2)}) collective-permute-start(f32[32,128]{1,0:T(8,128)S(1)} %get-tuple-element.61), channel_id=1, source_target_pairs={{0,32},{8,40},{16,48},{24,56},{32,0},{40,8},{48,16},{56,24},{1,33}... | collective-permute-start | bytes 49160 | tf_op jit(solution)/shard_map/ppermute | solution.py:29
  194.5 9.0 %collective-permute-start.11 = (f32[32,128]{1,0:T(8,128)S(1)}, f32[32,128]{1,0:T(8,128)S(1)}, u32[]{:S(2)}, u32[]{:S(2)}) collective-permute-start(f32[32,128]{1,0:T(8,128)S(1)} %get-tuple-element.67), channel_id=1, source_target_pairs={{0,8},{8,16},{16,24},{24,32},{32,40},{40,48},{48,56},{56,0},{1,9},... | collective-permute-start | bytes 49160 | tf_op jit(solution)/shard_map/ppermute | solution.py:29
  198.0 27.1 %collective-permute-start.17 = (f32[32,128]{1,0:T(8,128)S(1)}, f32[32,128]{1,0:T(8,128)S(1)}, u32[]{:S(2)}, u32[]{:S(2)}) collective-permute-start(f32[32,128]{1,0:T(8,128)S(1)} %get-tuple-element.66), channel_id=1, source_target_pairs={{0,56},{8,0},{16,8},{24,16},{32,24},{40,32},{48,40},{56,48},{1,57}... | collective-permute-start | bytes 49160 | tf_op jit(solution)/shard_map/ppermute | solution.py:29
  203.6 10.2 %collective-permute-start.13 = (f32[32,128]{1,0:T(8,128)S(1)}, f32[32,128]{1,0:T(8,128)S(1)}, u32[]{:S(2)}, u32[]{:S(2)}) collective-permute-start(f32[32,128]{1,0:T(8,128)S(1)} %get-tuple-element.69), channel_id=1, source_target_pairs={{0,24},{8,32},{16,40},{24,48},{32,56},{40,0},{48,8},{56,16},{1,25}... | collective-permute-start | bytes 49160 | tf_op jit(solution)/shard_map/ppermute | solution.py:29
  208.2 9.4 %collective-permute-start.14 = (f32[32,128]{1,0:T(8,128)S(1)}, f32[32,128]{1,0:T(8,128)S(1)}, u32[]{:S(2)}, u32[]{:S(2)}) collective-permute-start(f32[32,128]{1,0:T(8,128)S(1)} %get-tuple-element.70), channel_id=1, source_target_pairs={{0,32},{8,40},{16,48},{24,56},{32,0},{40,8},{48,16},{56,24},{1,33}... | collective-permute-start | bytes 49160 | tf_op jit(solution)/shard_map/ppermute | solution.py:29
  213.7 8.4 %collective-permute-start.15 = (f32[32,128]{1,0:T(8,128)S(1)}, f32[32,128]{1,0:T(8,128)S(1)}, u32[]{:S(2)}, u32[]{:S(2)}) collective-permute-start(f32[32,128]{1,0:T(8,128)S(1)} %get-tuple-element.71), channel_id=1, source_target_pairs={{0,40},{8,48},{16,56},{24,0},{32,8},{40,16},{48,24},{56,32},{1,41}... | collective-permute-start | bytes 49160 | tf_op jit(solution)/shard_map/ppermute | solution.py:29
  229.6 51.7 %collective-permute-start.20 = (f32[2,128,128]{2,1,0:T(8,128)}, f32[2,128,128]{2,1,0:T(8,128)}, u32[]{:S(2)}, u32[]{:S(2)}) collective-permute-start(f32[2,128,128]{2,1,0:T(8,128)} %get-tuple-element.51), channel_id=1, source_target_pairs={{0,6},{2,0},{4,2},{6,4},{1,7},{3,1},{5,3},{7,5},{8,14},{10,8},{12,... | collective-permute-start | bytes 393224 | tf_op jit(solution)/shard_map/ppermute | solution.py:29
  233.9 47.4 %collective-permute-start.19 = (f32[2,128,128]{2,1,0:T(8,128)S(1)}, f32[2,128,128]{2,1,0:T(8,128)}, u32[]{:S(2)}, u32[]{:S(2)}) collective-permute-start(f32[2,128,128]{2,1,0:T(8,128)S(1)} %get-tuple-element.52), channel_id=1, source_target_pairs={{0,4},{2,6},{4,0},{6,2},{1,5},{3,7},{5,1},{7,3},{8,12},{10,14},{12... | collective-permute-start | bytes 393224 | tf_op jit(solution)/shard_map/ppermute | solution.py:29
  236.9 44.4 %collective-permute-start.18 = (f32[2,128,128]{2,1,0:T(8,128)S(1)}, f32[2,128,128]{2,1,0:T(8,128)}, u32[]{:S(2)}, u32[]{:S(2)}) collective-permute-start(f32[2,128,128]{2,1,0:T(8,128)S(1)} %get-tuple-element.53), channel_id=1, source_target_pairs={{0,2},{2,4},{4,6},{6,0},{1,3},{3,5},{5,7},{7,1},{8,10},{10,12},{12... | collective-permute-start | bytes 393224 | tf_op jit(solution)/shard_map/ppermute | solution.py:29
  246.8 52.7 %collective-permute-start.57 = (bf16[8,4,8,32,128]{4,3,2,1,0:T(8,128)(2,1)S(1)}, bf16[8,4,8,32,128]{4,3,2,1,0:T(8,128)(2,1)}, u32[]{:S(2)}, u32[]{:S(2)}) collective-permute-start(bf16[8,4,8,32,128]{4,3,2,1,0:T(8,128)(2,1)S(1)} %broadcast_select_fusion), channel_id=1, source_target_pairs={{0,1},{1,0},{2,3},{3,2},{4,5},{5,4},{6,7},{7,6},{8,9},{9,8},{10,11... | collective-permute-start | bytes 6291464 | tf_op jit(solution)/shard_map/ppermute | solution.py:21
  279.3 23.7 %collective-permute-start.39 = (bf16[8,4,8,32,128]{4,3,0,1,2:T(8,128)(2,1)}, bf16[8,4,8,32,128]{4,3,0,1,2:T(8,128)(2,1)}, u32[]{:S(2)}, u32[]{:S(2)}) collective-permute-start(bf16[8,4,8,32,128]{4,3,0,1,2:T(8,128)(2,1)} %copy_select_fusion), channel_id=1, source_target_pairs={{0,1},{1,0},{2,3},{3,2},{4,5},{5,4},{6,7},{7,6},{8,9},{9,8},{10,11... | collective-permute-start | bytes 6291464 | tf_op jit(solution)/shard_map/ppermute | solution.py:21
  287.6 8.1 %collective-permute-start.21 = (f32[8,128,128]{2,1,0:T(8,128)}, f32[8,128,128]{2,1,0:T(8,128)}, u32[]{:S(2)}, u32[]{:S(2)}) collective-permute-start(f32[8,128,128]{2,1,0:T(8,128)} %bitcast.72), channel_id=1, source_target_pairs={{0,1},{1,0},{2,3},{3,2},{4,5},{5,4},{6,7},{7,6},{8,9},{9,8},{10,11... | collective-permute-start | bytes 1572872 | tf_op jit(solution)/shard_map/ppermute | solution.py:21
  (26 other events, 542.8 us)

commit v4 on v2

--- a/solution.py
+++ b/solution.py
@@ -22,22 +22,19 @@
 
 
 def prefix_of(own):
-    xi, ci = lax.axis_index("x"), lax.axis_index("c")
+    ci = lax.axis_index("c")
     nz, nx, nc = (lax.axis_size(a) for a in SEQ_AXES)
     assert nc == 2
     partner = swap_cores(own)
     chip_total = own + partner
     within_chip = jnp.where(ci == 1, partner, jnp.zeros_like(partner))
     half = HEADS // nc
-    quarter = half // nx
+    chips = nz * nx
     mine = lax.dynamic_slice_in_dim(chip_total, ci * half, half, 0)
-    by_chip = lax.all_to_all(mine.reshape(nx, quarter, HEAD, HEAD), "x", 0, 0)
-    before_in_row, row_total = exclusive_cumsum(by_chip)
-    pieces = row_total.reshape(nz, quarter * HEAD // nz, HEAD)
-    by_row = lax.all_to_all(pieces, "z", 0, 0)
-    before_rows, _ = exclusive_cumsum(by_row)
-    before_rows = lax.all_to_all(before_rows, "z", 0, 0).reshape(quarter, HEAD, HEAD)
-    back = lax.all_to_all(before_in_row + before_rows[None], "x", 0, 0)
+    pieces = mine.reshape(chips, half * HEAD // chips, HEAD)
+    by_chip = lax.all_to_all(pieces, ("z", "x"), 0, 0)
+    before, _ = exclusive_cumsum(by_chip)
+    back = lax.all_to_all(before, ("z", "x"), 0, 0)
     mine = back.reshape(half, HEAD, HEAD)
     theirs = swap_cores(mine)
     chip_prefix = jnp.where(
@@ -86,15 +83,12 @@
     normed = jnp.where(valid[:, None, None], normed, 0.0).astype(jnp.bfloat16)
     rows_per, cols_per = out_weight.shape
     ndp = lax.axis_size("dp")
-    ci = lax.axis_index("c")
-    wide = lax.all_gather(out_weight, "dp", axis=1, tiled=True)
-    own_rows = lax.all_gather(wide, ("z", "x"), axis=0, tiled=True)
-    other_rows = swap_cores(own_rows)
-    normed = normed.reshape(tok, nz, nx, nc, rows_per)
-    normed_own = jnp.take(normed, ci, axis=3).reshape(tok, nz * nx * rows_per)
-    normed_other = jnp.take(normed, 1 - ci, axis=3).reshape(tok, nz * nx * rows_per)
-    result = jnp.dot(normed_own, own_rows, preferred_element_type=jnp.float32)
-    result = result + jnp.dot(normed_other, other_rows, preferred_element_type=jnp.float32)
+    copies = jnp.broadcast_to(out_weight[None], (ndp, rows_per, cols_per))
+    by_column = lax.all_to_all(copies, "dp", 0, 0)
+    wide = jnp.transpose(by_column, (1, 0, 2)).reshape(rows_per, ndp * cols_per)
+    weight = lax.all_gather(wide, SEQ_AXES, axis=0, tiled=True)
+    normed = normed.reshape(tok, HEADS * HEAD)
+    result = jnp.dot(normed, weight, preferred_element_type=jnp.float32)
     return result.astype(jnp.bfloat16)[None]
 
 

time: 201 us -> 129 us (0.64)
  waiting for transfers between devices: 86.6 us -> 20.1 us
  starting transfers between devices: 29.8 us -> 10.4 us
  blocking collectives: 56 us -> 66.8 us
    all_gather x1, waiting for transfers between devices: 78.4 us -> 17.8 us  [body(): weight = lax.all_gather(wide, SEQ_AXES, axis=0, tiled=True)]
    all_to_all x3, blocking collectives: 33.2 us -> 66.8 us  [the longest x1 30.7 us: prefix_of(): by_chip = lax.all_to_all(pieces, ('z', 'x'), 0, 0)]
    all_gather x1 -> x0, blocking collectives: 22.8 us -> none  [body(): wide = lax.all_gather(out_weight, 'dp', axis=1, tiled=True)]
    ppermute x3 -> x2, starting transfers between devices: 25.8 us -> 10.4 us  [swap_cores(): return lax.ppermute(x, 'c', [(0, 1), (1, 0)])]
    all_to_all x1 -> x0, waiting for transfers between devices: 7.88 us -> none  [prefix_of(): lax.all_to_all(before_rows, 'z', 0, 0).reshape(quarter, HEAD, HEAD)]
    all_to_all x1 -> x0, starting transfers between devices: 4 us -> none  [prefix_of(): lax.all_to_all(before_rows, 'z', 0, 0).reshape(quarter, HEAD, HEAD)]
    dot_general x2 -> x1, matrix products: 4.47 us -> 5.46 us  [body(): result = jnp.dot(normed, weight, preferred_element_type=jnp.float32)]
  transfers between devices with their start and end apart: 5 -> 3, of which waited for: 3 -> 2; matrix products, arithmetic and copies ran while one was open for 5% -> 8% of each run, Pallas kernels for 0% -> 0%
where the time goes in v4:
time: 129 us; the launch traced here: 128 us
  blocking collectives  66.8 us (52%)
  waiting for transfers between devices  20.1 us (16%)
  between operations  14.2 us (11%)
  starting transfers between devices  10.4 us (8%)
  matrix products  9.05 us (7%)
  local copies, waits for them, and re-layouts  5.08 us (4%)
  other arithmetic  2.35 us (2%)
    all_to_all x1, blocking collectives, prefix_of(): by_chip = lax.all_to_all(pieces, ('z', 'x'), 0, 0)  30.7 us
    all_to_all x1, blocking collectives, prefix_of(): back = lax.all_to_all(before, ('z', 'x'), 0, 0)  20.7 us
    all_gather x1, waiting for transfers between devices, body(): weight = lax.all_gather(wide, SEQ_AXES, axis=0, tiled=True)  17.8 us
    all_to_all x1, blocking collectives, body(): by_column = lax.all_to_all(copies, 'dp', 0, 0)  15.4 us
    ppermute x2, starting transfers between devices, swap_cores(): return lax.ppermute(x, 'c', [(0, 1), (1, 0)])  10.4 us
    dot_general x1, matrix products, body(): result = jnp.dot(normed, weight, preferred_element_type=jnp.float32)  5.46 us
    dot_general x1, matrix products, body(): jnp.einsum('nthd,nhde->nthe', query_blocks.astype(jnp.float32), prior_sta...  2.67 us
  transfers between devices with their start and end apart: 3, of which 2 were waited for; matrix products, arithmetic and copies ran while one was open for 8% of the time, Pallas kernels for 0%

profile of v4, /device:TPU:1, one launch (start us, length us, event | category | flops | bytes accessed | tf_op | source)
XLA Modules:
  0.0 128.0 jit_solution(1714404033843367542)
XLA Ops:
  6.5 0.0 all-gather.2.cloned.1.call-start
  6.5 0.7 broadcast_in_dim.45
  7.3 15.4 %all_to_all.15 = bf16[8,32,256]{2,1,0:T(8,128)(2,1)S(1)} all-to-all(bf16[8,32,256]{2,1,0:T(8,128)(2,1)S(1)} %broadcast_in_dim.45), channel_id=1, replica_groups=mesh['dp'=8,'z'=8,'x'=4,'c'=2] {'dp'}, dimensions={0} | all-to-all | bytes 262144 | tf_op jit(solution)/shard_map/all_to_all | solution.py:87
  22.6 0.7 copy.27
  23.3 0.0 all-gather.2.cloned.1.call-update
  23.3 1.3 %copy.26 = bf16[1,128,2048]{1,2,0:T(8,128)(2,1)S(1)} copy(bf16[1,128,2048]{2,1,0:T(8,128)(2,1)} %param.7) | data formatting | bytes 1048576 | tf_op jit(solution)/shard_map/reshape.2
  24.6 1.1 copy.29
  25.8 0.0 copy-start.1
  25.8 0.3 fusion.20
  26.1 4.8 %collective-permute-start = (f32[16,128,128]{2,1,0:T(8,128)S(1)}, f32[16,128,128]{2,1,0:T(8,128)S(1)}, u32[]{:S(2)}, u32[]{:S(2)}) collective-permute-start(f32[16,128,128]{2,1,0:T(8,128)S(1)} %fusion.20), channel_id=1, source_target_pairs={{0,1},{1,0},{2,3},{3,2},{4,5},{5,4},{6,7},{7,6},{8,9},{9,8},{10,11... | collective-permute-start | bytes 3145736 | tf_op jit(solution)/shard_map/ppermute | solution.py:21
  31.0 2.3 %collective-permute-done = f32[16,128,128]{2,1,0:T(8,128)S(1)} collective-permute-done((f32[16,128,128]{2,1,0:T(8,128)S(1)}, f32[16,128,128]{2,1,0:T(8,128)S(1)}, u32[]{:S(2)}, u32[]{:S(2)}) %collective-permute-start) | collective-permute-done | bytes 1048608 | tf_op jit(solution)/shard_map/ppermute | solution.py:21
  33.2 0.0 copy-start
  33.2 0.1 dynamic-slice_add_fusion
  33.3 30.7 %all_to_all.16 = f32[32,32,128]{2,1,0:T(8,128)S(1)} all-to-all(f32[32,32,128]{2,1,0:T(8,128)S(1)} %bitcast.46), channel_id=1, replica_groups=mesh['dp'=8,'z'=8,'x'=4,'c'=2] {'z','x'}, dimensions={0} | all-to-all | bytes 1048576 | tf_op jit(solution)/shard_map/all_to_all | solution.py:35
  64.0 1.9 %fusion.28 = f32[32,32,128]{2,1,0:T(8,128)S(1)} fusion(f32[32,32,128]{2,1,0:T(8,128)S(1)} %all_to_all.16), kind=kOutput, calls=%fused_computation.37 | output fusion | flops 4063232 | bytes 1048576 | tf_op jit(solution)/shard_map/jit(cumsum)/reduce_window_sum | solution.py:16
  66.0 20.7 %all_to_all.17 = f32[32,32,128]{2,1,0:T(8,128)} all-to-all(f32[32,32,128]{2,1,0:T(8,128)S(1)} %concatenate.9), channel_id=1, replica_groups=mesh['dp'=8,'z'=8,'x'=4,'c'=2] {'z','x'}, dimensions={0} | all-to-all | bytes 1048576 | tf_op jit(solution)/shard_map/all_to_all | solution.py:37
  86.8 5.6 %collective-permute-start.1 = (f32[8,128,128]{2,1,0:T(8,128)}, f32[8,128,128]{2,1,0:T(8,128)S(1)}, u32[]{:S(2)}, u32[]{:S(2)}) collective-permute-start(f32[8,128,128]{2,1,0:T(8,128)} %bitcast.3), channel_id=1, source_target_pairs={{0,1},{1,0},{2,3},{3,2},{4,5},{5,4},{6,7},{7,6},{8,9},{9,8},{10,11... | collective-permute-start | bytes 1572872 | tf_op jit(solution)/shard_map/ppermute | solution.py:21
  92.3 1.1 copy.28
  94.2 0.0 copy-done
  94.2 0.6 convolution_bitcast_fusion
  94.8 0.0 collective-permute-done.1
  94.8 2.7 %fusion.12 = (f32[128,16]{0,1:T(8,128)S(1)}, f32[16,128,128]{2,1,0:T(8,128)S(1)}) fusion(f32[16,128,128]{2,1,0:T(8,128)S(1)} %convolution_bitcast_fusion, bf16[128,16,128]{2,1,0:T(8,128)(2,1)S(1)} %bitcast.45, f32[8,128,128]{2,1,0:T(8,128)S(1)} %collective-permute-done.1, f32[8,128,128]{2,1,0:T(8,128)} %bitcast.3, f32[16,128,128]{2,1,0:T(8,128)} %copy-done, ...), kind=kOutput, calls=%fused_computation.18 | convolution fusion | flops 404748288 | bytes 4726786 | tf_op jit(solution)/shard_map/nthd,nhde->nthe/dot_general | solution.py:74
  97.5 0.0 copy-done.1
  97.5 0.3 fusion.11
  97.9 17.8 %all-gather.2.cloned.1.call-done = bf16[2048,2048]{1,0:T(8,128)(2,1)} async-done(((bf16[32,2048]{1,0:T(8,128)(2,1)}), bf16[2048,2048]{1,0:T(8,128)(2,1)}) %all-gather.2.cloned.1.call-update) | async-done | bytes 8388624 | tf_op jit(solution)/shard_map/all_gather | solution.py:89
  115.7 5.5 %fusion = bf16[1,128,2048]{2,1,0:T(8,128)(2,1)} fusion(bf16[128,2048]{0,1:T(8,128)(2,1)S(1)} %fusion.11, bf16[2048,2048]{1,0:T(8,128)(2,1)} %all-gather.2.cloned.1.call-done), kind=kOutput, calls=%fused_computation.1 | convolution fusion | flops 1074003968 | bytes 9437184 | tf_op jit(solution)/shard_map/dot_general | solution.py:91
  (5 shorter events, 0.1 us)
Async XLA Ops:
  6.5 109.2 %all-gather.2.cloned.1.call-start = ((), (), s32[]{:S(2)}) async-start(), calls=%async_computation.3 | async-start | bytes 8519680 | tf_op jit(solution)/shard_map/all_gather | solution.py:89
  25.8 71.7 %copy-start.1 = (f32[2048]{0:T(1024)S(1)}, f32[2048]{0:T(1024)}, u32[]{:S(2)}) copy-start(f32[2048]{0:T(1024)} %param.10) | copy-start | bytes 24580
  26.1 7.1 %collective-permute-start = (f32[16,128,128]{2,1,0:T(8,128)S(1)}, f32[16,128,128]{2,1,0:T(8,128)S(1)}, u32[]{:S(2)}, u32[]{:S(2)}) collective-permute-start(f32[16,128,128]{2,1,0:T(8,128)S(1)} %fusion.20), channel_id=1, source_target_pairs={{0,1},{1,0},{2,3},{3,2},{4,5},{5,4},{6,7},{7,6},{8,9},{9,8},{10,11... | collective-permute-start | bytes 3145736 | tf_op jit(solution)/shard_map/ppermute | solution.py:21
  33.2 61.0 %copy-start = (f32[16,128,128]{2,1,0:T(8,128)}, f32[16,128,128]{2,1,0:T(8,128)S(1)}, u32[]{:S(2)}) copy-start(f32[16,128,128]{2,1,0:T(8,128)S(1)} %collective-permute-done) | copy-start | bytes 3145732
  86.8 8.1 %collective-permute-start.1 = (f32[8,128,128]{2,1,0:T(8,128)}, f32[8,128,128]{2,1,0:T(8,128)S(1)}, u32[]{:S(2)}, u32[]{:S(2)}) collective-permute-start(f32[8,128,128]{2,1,0:T(8,128)} %bitcast.3), channel_id=1, source_target_pairs={{0,1},{1,0},{2,3},{3,2},{4,5},{5,4},{6,7},{7,6},{8,9},{9,8},{10,11... | collective-permute-start | bytes 1572872 | tf_op jit(solution)/shard_map/ppermute | solution.py:21
Sparse Core Ops, SparseCore 0:
  23.4 92.1 all-gather.1

commit v5 on v4

--- a/solution.py
+++ b/solution.py
@@ -19,6 +19,22 @@
 
 def swap_cores(x):
     return lax.ppermute(x, "c", [(0, 1), (1, 0)])
+
+
+def doubling_gather(x, axis):
+    n, i = lax.axis_size(axis), lax.axis_index(axis)
+    block = x[None]
+    step = 1
+    while step < n:
+        partner = lax.ppermute(block, axis, [(j, j ^ step) for j in range(n)])
+        low = (i & step) == 0
+        block = jnp.where(
+            low,
+            jnp.concatenate([block, partner], axis=0),
+            jnp.concatenate([partner, block], axis=0),
+        )
+        step *= 2
+    return block
 
 
 def prefix_of(own):
@@ -83,8 +99,7 @@
     normed = jnp.where(valid[:, None, None], normed, 0.0).astype(jnp.bfloat16)
     rows_per, cols_per = out_weight.shape
     ndp = lax.axis_size("dp")
-    copies = jnp.broadcast_to(out_weight[None], (ndp, rows_per, cols_per))
-    by_column = lax.all_to_all(copies, "dp", 0, 0)
+    by_column = doubling_gather(out_weight, "dp")
     wide = jnp.transpose(by_column, (1, 0, 2)).reshape(rows_per, ndp * cols_per)
     weight = lax.all_gather(wide, SEQ_AXES, axis=0, tiled=True)
     normed = normed.reshape(tok, HEADS * HEAD)

time: 129 us -> 141 us (1.093)
  starting transfers between devices: 10.4 us -> 31.3 us
  blocking collectives: 66.8 us -> 49.3 us
  waiting for transfers between devices: 20.1 us -> 29.1 us
    ppermute x0 -> x3, starting transfers between devices: none -> 16.2 us  [doubling_gather(): partner = lax.ppermute(block, axis, [(j, j ^ step) for j in range(n)])]
    all_to_all x1 -> x0, blocking collectives: 15.4 us -> none  [body(): by_column = lax.all_to_all(copies, 'dp', 0, 0)]
    ppermute x2, starting transfers between devices: 10.4 us -> 15.1 us  [swap_cores(): return lax.ppermute(x, 'c', [(0, 1), (1, 0)])]
    all_gather x1, waiting for transfers between devices: 17.8 us -> 22.4 us  [body(): weight = lax.all_gather(wide, SEQ_AXES, axis=0, tiled=True)]
    ppermute x0 -> x3, waiting for transfers between devices: none -> 4.34 us  [doubling_gather(): partner = lax.ppermute(block, axis, [(j, j ^ step) for j in range(n)])]
    all_to_all x1, blocking collectives: 30.7 us -> 27.7 us  [prefix_of(): by_chip = lax.all_to_all(pieces, ('z', 'x'), 0, 0)]
  transfers between devices with their start and end apart: 3 -> 6, of which waited for: 2 -> 5; matrix products, arithmetic and copies ran while one was open for 8% -> 7% of each run, Pallas kernels for 0% -> 0%
where the time goes in v5:
time: 141 us
  blocking collectives  49.3 us (35%)
  starting transfers between devices  31.3 us (22%)
  waiting for transfers between devices  29.1 us (21%)
  between operations  14.2 us (10%)
  matrix products  9.15 us (6%)
  local copies, waits for them, and re-layouts  4.41 us (3%)
  other arithmetic  3.17 us (2%)
    all_to_all x1, blocking collectives, prefix_of(): by_chip = lax.all_to_all(pieces, ('z', 'x'), 0, 0)  27.7 us
    all_gather x1, waiting for transfers between devices, body(): weight = lax.all_gather(wide, SEQ_AXES, axis=0, tiled=True)  22.4 us
    all_to_all x1, blocking collectives, prefix_of(): back = lax.all_to_all(before, ('z', 'x'), 0, 0)  21.6 us
    ppermute x3, starting transfers between devices, doubling_gather(): partner = lax.ppermute(block, axis, [(j, j ^ step) for j in range(n)])  16.2 us
    ppermute x2, starting transfers between devices, swap_cores(): return lax.ppermute(x, 'c', [(0, 1), (1, 0)])  15.1 us
    dot_general x1, matrix products, body(): result = jnp.dot(normed, weight, preferred_element_type=jnp.float32)  5.45 us
    ppermute x3, waiting for transfers between devices, doubling_gather(): partner = lax.ppermute(block, axis, [(j, j ^ step) for j in range(n)])  4.34 us
  transfers between devices with their start and end apart: 6, of which 5 were waited for; matrix products, arithmetic and copies ran while one was open for 7% of the time, Pallas kernels for 0%

profile of v5, /device:TPU:1, one launch (start us, length us, event | category | flops | bytes accessed | tf_op | source)
XLA Modules:
  0.0 140.6 jit_solution(10446351791778074090)
XLA Ops:
  6.5 0.0 all-gather.2.cloned.1.call-start
  6.5 4.0 %collective-permute-start.2 = (bf16[1,32,256]{2,1,0:T(8,128)(2,1)}, bf16[1,32,256]{2,1,0:T(8,128)(2,1)S(1)}, u32[]{:S(2)}, u32[]{:S(2)}) collective-permute-start(bf16[1,32,256]{2,1,0:T(8,128)(2,1)} %bitcast.52), channel_id=1, source_target_pairs={{0,64},{64,0},{128,192},{192,128},{256,320},{320,256},{384,448},{4... | collective-permute-start | bytes 49160 | tf_op jit(solution)/shard_map/ppermute | solution.py:29
  10.6 1.3 collective-permute-done.2
  11.9 0.8 maximum_select_fusion.3
  12.7 4.4 %collective-permute-start.3 = (bf16[2,32,256]{2,1,0:T(8,128)(2,1)S(1)}, bf16[2,32,256]{2,1,0:T(8,128)(2,1)S(1)}, u32[]{:S(2)}, u32[]{:S(2)}) collective-permute-start(bf16[2,32,256]{2,1,0:T(8,128)(2,1)S(1)} %maximum_select_fusion.3), channel_id=1, source_target_pairs={{0,128},{64,192},{128,0},{192,64},{256,384},{320,448},{384,256},{4... | collective-permute-start | bytes 98312 | tf_op jit(solution)/shard_map/ppermute | solution.py:29
  17.1 1.3 collective-permute-done.3
  18.4 7.8 %collective-permute-start.4 = (bf16[4,32,256]{2,1,0:T(8,128)(2,1)S(1)}, bf16[4,32,256]{2,1,0:T(8,128)(2,1)S(1)}, u32[]{:S(2)}, u32[]{:S(2)}) collective-permute-start(bf16[4,32,256]{2,1,0:T(8,128)(2,1)S(1)} %maximum_select_fusion.2), channel_id=1, source_target_pairs={{0,256},{64,320},{128,384},{192,448},{256,0},{320,64},{384,128},{4... | collective-permute-start | bytes 196616 | tf_op jit(solution)/shard_map/ppermute | solution.py:29
  26.2 1.7 %collective-permute-done.4 = bf16[4,32,256]{2,1,0:T(8,128)(2,1)S(1)} collective-permute-done((bf16[4,32,256]{2,1,0:T(8,128)(2,1)S(1)}, bf16[4,32,256]{2,1,0:T(8,128)(2,1)S(1)}, u32[]{:S(2)}, u32[]{:S(2)}) %collective-permute-start.4) | collective-permute-done | bytes 65568 | tf_op jit(solution)/shard_map/ppermute | solution.py:29
  28.0 0.7 copy.20
  28.6 0.0 all-gather.2.cloned.1.call-update
  28.7 1.3 copy.19
  30.0 1.1 copy.22
  31.1 0.0 copy-start.1
  31.1 0.3 fusion.23
  31.4 10.7 %collective-permute-start = (f32[16,128,128]{2,1,0:T(8,128)S(1)}, f32[16,128,128]{2,1,0:T(8,128)S(1)}, u32[]{:S(2)}, u32[]{:S(2)}) collective-permute-start(f32[16,128,128]{2,1,0:T(8,128)S(1)} %fusion.23), channel_id=1, source_target_pairs={{0,1},{1,0},{2,3},{3,2},{4,5},{5,4},{6,7},{7,6},{8,9},{9,8},{10,11... | collective-permute-start | bytes 3145736 | tf_op jit(solution)/shard_map/ppermute | solution.py:21
  42.2 2.3 %collective-permute-done = f32[16,128,128]{2,1,0:T(8,128)S(1)} collective-permute-done((f32[16,128,128]{2,1,0:T(8,128)S(1)}, f32[16,128,128]{2,1,0:T(8,128)S(1)}, u32[]{:S(2)}, u32[]{:S(2)}) %collective-permute-start) | collective-permute-done | bytes 1048608 | tf_op jit(solution)/shard_map/ppermute | solution.py:21
  44.5 0.0 copy-start
  44.5 0.1 dynamic-slice_add_fusion
  44.5 27.7 %all_to_all.10 = f32[32,32,128]{2,1,0:T(8,128)S(1)} all-to-all(f32[32,32,128]{2,1,0:T(8,128)S(1)} %bitcast.48), channel_id=1, replica_groups=mesh['dp'=8,'z'=8,'x'=4,'c'=2] {'z','x'}, dimensions={0} | all-to-all | bytes 1048576 | tf_op jit(solution)/shard_map/all_to_all | solution.py:51
  72.2 1.9 %fusion.29 = f32[32,32,128]{2,1,0:T(8,128)S(1)} fusion(f32[32,32,128]{2,1,0:T(8,128)S(1)} %all_to_all.10), kind=kOutput, calls=%fused_computation.41 | output fusion | flops 4063232 | bytes 1048576 | tf_op jit(solution)/shard_map/jit(cumsum)/reduce_window_sum | solution.py:16
  74.3 21.6 %all_to_all.11 = f32[32,32,128]{2,1,0:T(8,128)} all-to-all(f32[32,32,128]{2,1,0:T(8,128)S(1)} %concatenate.27), channel_id=1, replica_groups=mesh['dp'=8,'z'=8,'x'=4,'c'=2] {'z','x'}, dimensions={0} | all-to-all | bytes 1048576 | tf_op jit(solution)/shard_map/all_to_all | solution.py:53
  95.9 4.3 %collective-permute-start.1 = (f32[8,128,128]{2,1,0:T(8,128)}, f32[8,128,128]{2,1,0:T(8,128)S(1)}, u32[]{:S(2)}, u32[]{:S(2)}) collective-permute-start(f32[8,128,128]{2,1,0:T(8,128)} %bitcast.4), channel_id=1, source_target_pairs={{0,1},{1,0},{2,3},{3,2},{4,5},{5,4},{6,7},{7,6},{8,9},{9,8},{10,11... | collective-permute-start | bytes 1572872 | tf_op jit(solution)/shard_map/ppermute | solution.py:21
  100.2 1.2 copy.21
  102.1 0.0 copy-done
  102.1 0.6 convolution_bitcast_fusion
  102.7 0.0 collective-permute-done.1
  102.8 2.8 %fusion.12 = (f32[128,16]{0,1:T(8,128)S(1)}, f32[16,128,128]{2,1,0:T(8,128)S(1)}) fusion(f32[16,128,128]{2,1,0:T(8,128)S(1)} %convolution_bitcast_fusion, bf16[128,16,128]{2,1,0:T(8,128)(2,1)S(1)} %bitcast.47, f32[8,128,128]{2,1,0:T(8,128)S(1)} %collective-permute-done.1, f32[8,128,128]{2,1,0:T(8,128)} %bitcast.4, f32[16,128,128]{2,1,0:T(8,128)} %copy-done, ...), kind=kOutput, calls=%fused_computation.18 | convolution fusion | flops 404748288 | bytes 4726786 | tf_op jit(solution)/shard_map/nthd,nhde->nthe/dot_general | solution.py:90
  105.5 0.0 copy-done.1
  105.6 0.3 fusion.11
  105.9 22.4 %all-gather.2.cloned.1.call-done = bf16[2048,2048]{1,0:T(8,128)(2,1)} async-done(((bf16[32,2048]{1,0:T(8,128)(2,1)}), bf16[2048,2048]{1,0:T(8,128)(2,1)}) %all-gather.2.cloned.1.call-update) | async-done | bytes 8388624 | tf_op jit(solution)/shard_map/all_gather | solution.py:104
  128.3 5.5 %fusion = bf16[1,128,2048]{2,1,0:T(8,128)(2,1)} fusion(bf16[128,2048]{0,1:T(8,128)(2,1)S(1)} %fusion.11, bf16[2048,2048]{1,0:T(8,128)(2,1)} %all-gather.2.cloned.1.call-done), kind=kOutput, calls=%fused_computation.1 | convolution fusion | flops 1074003968 | bytes 9437184 | tf_op jit(solution)/shard_map/dot_general | solution.py:106
  (7 shorter events, 0.1 us)
Async XLA Ops:
  6.5 121.8 %all-gather.2.cloned.1.call-start = ((), (), s32[]{:S(2)}) async-start(), calls=%async_computation.2 | async-start | bytes 8519680 | tf_op jit(solution)/shard_map/all_gather | solution.py:104
  6.5 5.3 %collective-permute-start.2 = (bf16[1,32,256]{2,1,0:T(8,128)(2,1)}, bf16[1,32,256]{2,1,0:T(8,128)(2,1)S(1)}, u32[]{:S(2)}, u32[]{:S(2)}) collective-permute-start(bf16[1,32,256]{2,1,0:T(8,128)(2,1)} %bitcast.52), channel_id=1, source_target_pairs={{0,64},{64,0},{128,192},{192,128},{256,320},{320,256},{384,448},{4... | collective-permute-start | bytes 49160 | tf_op jit(solution)/shard_map/ppermute | solution.py:29
  12.7 5.7 %collective-permute-start.3 = (bf16[2,32,256]{2,1,0:T(8,128)(2,1)S(1)}, bf16[2,32,256]{2,1,0:T(8,128)(2,1)S(1)}, u32[]{:S(2)}, u32[]{:S(2)}) collective-permute-start(bf16[2,32,256]{2,1,0:T(8,128)(2,1)S(1)} %maximum_select_fusion.3), channel_id=1, source_target_pairs={{0,128},{64,192},{128,0},{192,64},{256,384},{320,448},{384,256},{4... | collective-permute-start | bytes 98312 | tf_op jit(solution)/shard_map/ppermute | solution.py:29
  18.4 9.6 %collective-permute-start.4 = (bf16[4,32,256]{2,1,0:T(8,128)(2,1)S(1)}, bf16[4,32,256]{2,1,0:T(8,128)(2,1)S(1)}, u32[]{:S(2)}, u32[]{:S(2)}) collective-permute-start(bf16[4,32,256]{2,1,0:T(8,128)(2,1)S(1)} %maximum_select_fusion.2), channel_id=1, source_target_pairs={{0,256},{64,320},{128,384},{192,448},{256,0},{320,64},{384,128},{4... | collective-permute-start | bytes 196616 | tf_op jit(solution)/shard_map/ppermute | solution.py:29
  31.1 74.4 %copy-start.1 = (f32[2048]{0:T(1024)S(1)}, f32[2048]{0:T(1024)}, u32[]{:S(2)}) copy-start(f32[2048]{0:T(1024)} %param.10) | copy-start | bytes 24580
  31.4 13.0 %collective-permute-start = (f32[16,128,128]{2,1,0:T(8,128)S(1)}, f32[16,128,128]{2,1,0:T(8,128)S(1)}, u32[]{:S(2)}, u32[]{:S(2)}) collective-permute-start(f32[16,128,128]{2,1,0:T(8,128)S(1)} %fusion.23), channel_id=1, source_target_pairs={{0,1},{1,0},{2,3},{3,2},{4,5},{5,4},{6,7},{7,6},{8,9},{9,8},{10,11... | collective-permute-start | bytes 3145736 | tf_op jit(solution)/shard_map/ppermute | solution.py:21
  44.5 57.7 %copy-start = (f32[16,128,128]{2,1,0:T(8,128)}, f32[16,128,128]{2,1,0:T(8,128)S(1)}, u32[]{:S(2)}) copy-start(f32[16,128,128]{2,1,0:T(8,128)S(1)} %collective-permute-done) | copy-start | bytes 3145732
  95.9 6.9 %collective-permute-start.1 = (f32[8,128,128]{2,1,0:T(8,128)}, f32[8,128,128]{2,1,0:T(8,128)S(1)}, u32[]{:S(2)}, u32[]{:S(2)}) collective-permute-start(f32[8,128,128]{2,1,0:T(8,128)} %bitcast.4), channel_id=1, source_target_pairs={{0,1},{1,0},{2,3},{3,2},{4,5},{5,4},{6,7},{7,6},{8,9},{9,8},{10,11... | collective-permute-start | bytes 1572872 | tf_op jit(solution)/shard_map/ppermute | solution.py:21
Sparse Core Ops, SparseCore 0:
  28.8 99.5 all-gather.1

commit v6 on v4

--- a/solution.py
+++ b/solution.py
@@ -83,10 +83,15 @@
     normed = jnp.where(valid[:, None, None], normed, 0.0).astype(jnp.bfloat16)
     rows_per, cols_per = out_weight.shape
     ndp = lax.axis_size("dp")
-    copies = jnp.broadcast_to(out_weight[None], (ndp, rows_per, cols_per))
-    by_column = lax.all_to_all(copies, "dp", 0, 0)
-    wide = jnp.transpose(by_column, (1, 0, 2)).reshape(rows_per, ndp * cols_per)
-    weight = lax.all_gather(wide, SEQ_AXES, axis=0, tiled=True)
+    by_row = lax.all_to_all(
+        jnp.broadcast_to(out_weight[None], (nz, rows_per, cols_per)), "z", 0, 0
+    )
+    by_column = lax.all_to_all(
+        jnp.broadcast_to(by_row[None], (ndp, nz, rows_per, cols_per)), "dp", 0, 0
+    )
+    block = jnp.transpose(by_column, (1, 2, 0, 3)).reshape(nz * rows_per, ndp * cols_per)
+    weight = lax.all_gather(block, ("x", "c"), axis=0, tiled=True)
+    normed = normed.reshape(tok, nz, nx, nc, rows_per).transpose(0, 2, 3, 1, 4)
     normed = normed.reshape(tok, HEADS * HEAD)
     result = jnp.dot(normed, weight, preferred_element_type=jnp.float32)
     return result.astype(jnp.bfloat16)[None]

time: 129 us -> 137 us (1.062)
  blocking collectives: 66.8 us -> 92.4 us
  waiting for transfers between devices: 20.1 us -> 2.3 us
    all_to_all x1 -> x2, blocking collectives: 15.4 us -> 50.8 us  [the longest x1 32.4 us: body(): lax.all_to_all(jnp.broadcast_to(by_row[None], (ndp, nz, rows_per, cols_pe...]
    all_gather x1, waiting for transfers between devices: 17.8 us -> 0.02 us  [body(): weight = lax.all_gather(block, ('x', 'c'), axis=0, tiled=True)]
    all_to_all x1, blocking collectives: 30.7 us -> 21.6 us  [prefix_of(): by_chip = lax.all_to_all(pieces, ('z', 'x'), 0, 0)]
  transfers between devices with their start and end apart: 3 -> 3, of which waited for: 2 -> 1; matrix products, arithmetic and copies ran while one was open for 8% -> 6% of each run, Pallas kernels for 0% -> 0%
where the time goes in v6:
time: 137 us; the launch traced here: 136 us
  blocking collectives  92.4 us (67%)
  between operations  14.3 us (10%)
  starting transfers between devices  11.3 us (8%)
  matrix products  9.03 us (7%)
  local copies, waits for them, and re-layouts  4.63 us (3%)
  other arithmetic  2.36 us (2%)
  waiting for transfers between devices  2.3 us (2%)
    all_to_all x1, blocking collectives, body(): lax.all_to_all(jnp.broadcast_to(by_row[None], (ndp, nz, rows_per, cols_pe...  32.4 us
    all_to_all x1, blocking collectives, prefix_of(): by_chip = lax.all_to_all(pieces, ('z', 'x'), 0, 0)  21.6 us
    all_to_all x1, blocking collectives, prefix_of(): back = lax.all_to_all(before, ('z', 'x'), 0, 0)  20.1 us
    all_to_all x1, blocking collectives, body(): lax.all_to_all(jnp.broadcast_to(out_weight[None], (nz, rows_per, cols_per...  18.4 us
    ppermute x2, starting transfers between devices, swap_cores(): return lax.ppermute(x, 'c', [(0, 1), (1, 0)])  11.3 us
    dot_general x1, matrix products, body(): result = jnp.dot(normed, weight, preferred_element_type=jnp.float32)  5.46 us
  transfers between devices with their start and end apart: 3, of which 1 were waited for; matrix products, arithmetic and copies ran while one was open for 6% of the time, Pallas kernels for 0%

profile of v6, /device:TPU:1, one launch (start us, length us, event | category | flops | bytes accessed | tf_op | source)
XLA Modules:
  0.0 136.3 jit_solution(7662155949841135370)
XLA Ops:
  6.5 0.0 copy-start.1
  6.5 0.0 copy-start.2
  6.5 0.0 all-gather.2.cloned.1.call-start
  6.5 0.8 broadcast_in_dim.51
  7.4 18.4 %all_to_all.20 = bf16[8,32,256]{2,1,0:T(8,128)(2,1)S(1)} all-to-all(bf16[8,32,256]{2,1,0:T(8,128)(2,1)S(1)} %broadcast_in_dim.51), channel_id=1, replica_groups=mesh['dp'=8,'z'=8,'x'=4,'c'=2] {'z'}, dimensions={0} | all-to-all | bytes 262144 | tf_op jit(solution)/shard_map/all_to_all | solution.py:86
  25.8 0.1 broadcast_in_dim.52
  25.9 32.4 %all_to_all.21 = bf16[8,8,32,256]{3,2,1,0:T(8,128)(2,1)S(1)} all-to-all(bf16[8,8,32,256]{3,2,1,0:T(8,128)(2,1)S(1)} %broadcast_in_dim.52), channel_id=1, replica_groups=mesh['dp'=8,'z'=8,'x'=4,'c'=2] {'dp'}, dimensions={0} | all-to-all | bytes 2097152 | tf_op jit(solution)/shard_map/all_to_all | solution.py:89
  58.2 0.0 copy-start.3
  58.2 0.6 copy.38
  58.9 1.4 copy.43
  60.2 0.0 all-gather.2.cloned.1.call-update
  60.2 0.0 copy-done.1
  60.3 0.3 copy.40
  60.5 0.0 copy-done.2
  60.5 0.1 copy.42
  60.7 0.3 fusion.20
  61.0 5.9 %collective-permute-start = (f32[16,128,128]{2,1,0:T(8,128)S(1)}, f32[16,128,128]{2,1,0:T(8,128)S(1)}, u32[]{:S(2)}, u32[]{:S(2)}) collective-permute-start(f32[16,128,128]{2,1,0:T(8,128)S(1)} %fusion.20), channel_id=1, source_target_pairs={{0,1},{1,0},{2,3},{3,2},{4,5},{5,4},{6,7},{7,6},{8,9},{9,8},{10,11... | collective-permute-start | bytes 3145736 | tf_op jit(solution)/shard_map/ppermute | solution.py:21
  66.8 2.3 %collective-permute-done = f32[16,128,128]{2,1,0:T(8,128)S(1)} collective-permute-done((f32[16,128,128]{2,1,0:T(8,128)S(1)}, f32[16,128,128]{2,1,0:T(8,128)S(1)}, u32[]{:S(2)}, u32[]{:S(2)}) %collective-permute-start) | collective-permute-done | bytes 1048608 | tf_op jit(solution)/shard_map/ppermute | solution.py:21
  69.1 0.0 copy-start
  69.1 0.1 dynamic-slice_add_fusion
  69.2 21.6 %all_to_all.22 = f32[32,32,128]{2,1,0:T(8,128)S(1)} all-to-all(f32[32,32,128]{2,1,0:T(8,128)S(1)} %bitcast.47), channel_id=1, replica_groups=mesh['dp'=8,'z'=8,'x'=4,'c'=2] {'z','x'}, dimensions={0} | all-to-all | bytes 1048576 | tf_op jit(solution)/shard_map/all_to_all | solution.py:35
  90.7 1.9 %fusion.28 = f32[32,32,128]{2,1,0:T(8,128)S(1)} fusion(f32[32,32,128]{2,1,0:T(8,128)S(1)} %all_to_all.22), kind=kOutput, calls=%fused_computation.37 | output fusion | flops 4063232 | bytes 1048576 | tf_op jit(solution)/shard_map/jit(cumsum)/reduce_window_sum | solution.py:16
  92.7 20.1 %all_to_all.23 = f32[32,32,128]{2,1,0:T(8,128)} all-to-all(f32[32,32,128]{2,1,0:T(8,128)S(1)} %concatenate.9), channel_id=1, replica_groups=mesh['dp'=8,'z'=8,'x'=4,'c'=2] {'z','x'}, dimensions={0} | all-to-all | bytes 1048576 | tf_op jit(solution)/shard_map/all_to_all | solution.py:37
  112.8 5.5 %collective-permute-start.1 = (f32[8,128,128]{2,1,0:T(8,128)}, f32[8,128,128]{2,1,0:T(8,128)S(1)}, u32[]{:S(2)}, u32[]{:S(2)}) collective-permute-start(f32[8,128,128]{2,1,0:T(8,128)} %bitcast.3), channel_id=1, source_target_pairs={{0,1},{1,0},{2,3},{3,2},{4,5},{5,4},{6,7},{7,6},{8,9},{9,8},{10,11... | collective-permute-start | bytes 1572872 | tf_op jit(solution)/shard_map/ppermute | solution.py:21
  118.3 1.1 copy.41
  120.1 0.0 copy-done.3
  120.1 0.1 mul.49
  120.3 0.0 copy-done
  120.3 0.6 convolution_bitcast_fusion
  120.9 0.0 collective-permute-done.1
  120.9 2.7 %fusion.9 = (f32[128,16]{0,1:T(8,128)S(1)}, f32[16,128,128]{2,1,0:T(8,128)S(1)}) fusion(f32[16,128,128]{2,1,0:T(8,128)S(1)} %convolution_bitcast_fusion, bf16[128,16,128]{2,1,0:T(8,128)(2,1)S(1)} %bitcast.41, f32[8,128,128]{2,1,0:T(8,128)S(1)} %collective-permute-done.1, f32[8,128,128]{2,1,0:T(8,128)} %bitcast.3, f32[16,128,128]{2,1,0:T(8,128)} %copy-done, ...), kind=kOutput, calls=%fused_computation.14 | convolution fusion | flops 404748288 | bytes 4726786 | tf_op jit(solution)/shard_map/nthd,nhde->nthe/dot_general | solution.py:74
  123.6 0.3 fusion.12
  123.9 0.0 all-gather.2.cloned.1.call-done
  124.0 5.5 %fusion = bf16[1,128,2048]{2,1,0:T(8,128)(2,1)} fusion(bf16[128,2048]{0,1:T(8,128)(2,1)S(1)} %bitcast.42, bf16[2048,2048]{1,0:T(8,128)(2,1)} %all-gather.2.cloned.1.call-done), kind=kOutput, calls=%fused_computation.1 | convolution fusion | flops 1074003968 | bytes 9437184 | tf_op jit(solution)/shard_map/dot_general | solution.py:96
  (8 shorter events, 0.1 us)
Async XLA Ops:
  6.5 53.7 %copy-start.1 = (bf16[1,128,2048]{2,1,0:T(8,128)(2,1)S(1)}, bf16[1,128,2048]{2,1,0:T(8,128)(2,1)}, u32[]{:S(2)}) copy-start(bf16[1,128,2048]{2,1,0:T(8,128)(2,1)} %param.7) | copy-start | bytes 1572868
  6.5 54.0 %copy-start.2 = (bf16[1,128,2048]{2,1,0:T(8,128)(2,1)S(1)}, bf16[1,128,2048]{2,1,0:T(8,128)(2,1)}, u32[]{:S(2)}) copy-start(bf16[1,128,2048]{2,1,0:T(8,128)(2,1)} %param.8) | copy-start | bytes 1572868
  6.5 117.4 %all-gather.2.cloned.1.call-start = ((), (), s32[]{:S(2)}) async-start(), calls=%async_computation.4 | async-start | bytes 9437184 | tf_op jit(solution)/shard_map/all_gather | solution.py:93
  58.2 61.9 %copy-start.3 = (f32[2048]{0:T(1024)S(1)}, f32[2048]{0:T(1024)}, u32[]{:S(2)}) copy-start(f32[2048]{0:T(1024)} %param.10) | copy-start | bytes 24580
  61.0 8.1 %collective-permute-start = (f32[16,128,128]{2,1,0:T(8,128)S(1)}, f32[16,128,128]{2,1,0:T(8,128)S(1)}, u32[]{:S(2)}, u32[]{:S(2)}) collective-permute-start(f32[16,128,128]{2,1,0:T(8,128)S(1)} %fusion.20), channel_id=1, source_target_pairs={{0,1},{1,0},{2,3},{3,2},{4,5},{5,4},{6,7},{7,6},{8,9},{9,8},{10,11... | collective-permute-start | bytes 3145736 | tf_op jit(solution)/shard_map/ppermute | solution.py:21
  69.1 51.2 %copy-start = (f32[16,128,128]{2,1,0:T(8,128)}, f32[16,128,128]{2,1,0:T(8,128)S(1)}, u32[]{:S(2)}) copy-start(f32[16,128,128]{2,1,0:T(8,128)S(1)} %collective-permute-done) | copy-start | bytes 3145732
  112.8 8.1 %collective-permute-start.1 = (f32[8,128,128]{2,1,0:T(8,128)}, f32[8,128,128]{2,1,0:T(8,128)S(1)}, u32[]{:S(2)}, u32[]{:S(2)}) collective-permute-start(f32[8,128,128]{2,1,0:T(8,128)} %bitcast.3), channel_id=1, source_target_pairs={{0,1},{1,0},{2,3},{3,2},{4,5},{5,4},{6,7},{7,6},{8,9},{9,8},{10,11... | collective-permute-start | bytes 1572872 | tf_op jit(solution)/shard_map/ppermute | solution.py:21
Sparse Core Ops, SparseCore 0:
  60.4 61.5 all-gather.1

commit v7 on v4

--- a/solution.py
+++ b/solution.py
@@ -83,10 +83,11 @@
     normed = jnp.where(valid[:, None, None], normed, 0.0).astype(jnp.bfloat16)
     rows_per, cols_per = out_weight.shape
     ndp = lax.axis_size("dp")
-    copies = jnp.broadcast_to(out_weight[None], (ndp, rows_per, cols_per))
-    by_column = lax.all_to_all(copies, "dp", 0, 0)
-    wide = jnp.transpose(by_column, (1, 0, 2)).reshape(rows_per, ndp * cols_per)
-    weight = lax.all_gather(wide, SEQ_AXES, axis=0, tiled=True)
+    copies = jnp.broadcast_to(out_weight[None], (nz * ndp, rows_per, cols_per))
+    by_peer = lax.all_to_all(copies, ("z", "dp"), 0, 0).reshape(nz, ndp, rows_per, cols_per)
+    block = jnp.transpose(by_peer, (0, 2, 1, 3)).reshape(nz * rows_per, ndp * cols_per)
+    weight = lax.all_gather(block, ("x", "c"), axis=0, tiled=True)
+    normed = normed.reshape(tok, nz, nx, nc, rows_per).transpose(0, 2, 3, 1, 4)
     normed = normed.reshape(tok, HEADS * HEAD)
     result = jnp.dot(normed, weight, preferred_element_type=jnp.float32)
     return result.astype(jnp.bfloat16)[None]

time: 129 us -> 131 us (1.016)
  blocking collectives: 66.8 us -> 87.7 us
  waiting for transfers between devices: 20.1 us -> 2.3 us
    all_to_all x1, blocking collectives: 15.4 us -> 44.4 us  [body(): lax.all_to_all(copies, ('z', 'dp'), 0, 0)]
    all_gather x1, waiting for transfers between devices: 17.8 us -> 0.02 us  [body(): weight = lax.all_gather(block, ('x', 'c'), axis=0, tiled=True)]
    all_to_all x1, blocking collectives: 30.7 us -> 23.2 us  [prefix_of(): by_chip = lax.all_to_all(pieces, ('z', 'x'), 0, 0)]
    unnamed x6 -> x11, local copies, waits for them, and re-layouts: 2.31 us -> 2.64 us
  transfers between devices with their start and end apart: 3 -> 3, of which waited for: 2 -> 1; matrix products, arithmetic and copies ran while one was open for 8% -> 6% of each run, Pallas kernels for 0% -> 0%
where the time goes in v7:
time: 131 us
  blocking collectives  87.7 us (67%)
  between operations  14.2 us (11%)
  starting transfers between devices  10.6 us (8%)
  matrix products  9.12 us (7%)
  local copies, waits for them, and re-layouts  4.63 us (4%)
  other arithmetic  2.36 us (2%)
  waiting for transfers between devices  2.3 us (2%)
    all_to_all x1, blocking collectives, body(): lax.all_to_all(copies, ('z', 'dp'), 0, 0)  44.4 us
    all_to_all x1, blocking collectives, prefix_of(): by_chip = lax.all_to_all(pieces, ('z', 'x'), 0, 0)  23.2 us
    all_to_all x1, blocking collectives, prefix_of(): back = lax.all_to_all(before, ('z', 'x'), 0, 0)  20.1 us
    ppermute x2, starting transfers between devices, swap_cores(): return lax.ppermute(x, 'c', [(0, 1), (1, 0)])  10.6 us
    dot_general x1, matrix products, body(): result = jnp.dot(normed, weight, preferred_element_type=jnp.float32)  5.46 us
    dot_general x1, matrix products, body(): jnp.einsum('nthd,nhde->nthe', query_blocks.astype(jnp.float32), prior_sta...  2.75 us
    unnamed x11, local copies, waits for them, and re-layouts  2.64 us
  transfers between devices with their start and end apart: 3, of which 1 were waited for; matrix products, arithmetic and copies ran while one was open for 6% of the time, Pallas kernels for 0%

profile of v7, /device:TPU:1, one launch (start us, length us, event | category | flops | bytes accessed | tf_op | source)
XLA Modules:
  0.0 130.9 jit_solution(17135851832509490183)
XLA Ops:
  6.5 0.0 copy-start.1
  6.5 0.0 copy-start.2
  6.5 0.0 all-gather.2.cloned.1.call-start
  6.5 0.9 broadcast_in_dim.45
  7.5 44.4 %all_to_all.15 = bf16[64,32,256]{2,1,0:T(8,128)(2,1)S(1)} all-to-all(bf16[64,32,256]{2,1,0:T(8,128)(2,1)S(1)} %broadcast_in_dim.45), channel_id=1, replica_groups=mesh['dp'=8,'z'=8,'x'=4,'c'=2] {'z','dp'}, dimensions={0} | all-to-all | bytes 2097152 | tf_op jit(solution)/shard_map/all_to_all | solution.py:87
  51.9 0.0 copy-start.3
  51.9 0.6 copy.28
  52.5 1.4 %copy.33 = bf16[32,8,8,256]{3,1,2,0:T(8,128)(2,1)} copy(bf16[32,8,8,256]{3,2,1,0:T(8,128)(2,1)S(1)} %bitcast.47) | data formatting | bytes 2097152
  53.9 0.0 all-gather.2.cloned.1.call-update
  53.9 0.0 copy-done.1
  53.9 0.3 copy.30
  54.2 0.0 copy-done.2
  54.2 0.1 copy.32
  54.3 0.3 fusion.20
  54.6 5.1 %collective-permute-start = (f32[16,128,128]{2,1,0:T(8,128)S(1)}, f32[16,128,128]{2,1,0:T(8,128)S(1)}, u32[]{:S(2)}, u32[]{:S(2)}) collective-permute-start(f32[16,128,128]{2,1,0:T(8,128)S(1)} %fusion.20), channel_id=1, source_target_pairs={{0,1},{1,0},{2,3},{3,2},{4,5},{5,4},{6,7},{7,6},{8,9},{9,8},{10,11... | collective-permute-start | bytes 3145736 | tf_op jit(solution)/shard_map/ppermute | solution.py:21
  59.8 2.3 %collective-permute-done = f32[16,128,128]{2,1,0:T(8,128)S(1)} collective-permute-done((f32[16,128,128]{2,1,0:T(8,128)S(1)}, f32[16,128,128]{2,1,0:T(8,128)S(1)}, u32[]{:S(2)}, u32[]{:S(2)}) %collective-permute-start) | collective-permute-done | bytes 1048608 | tf_op jit(solution)/shard_map/ppermute | solution.py:21
  62.0 0.0 copy-start
  62.0 0.1 dynamic-slice_add_fusion
  62.1 23.2 %all_to_all.16 = f32[32,32,128]{2,1,0:T(8,128)S(1)} all-to-all(f32[32,32,128]{2,1,0:T(8,128)S(1)} %bitcast.49), channel_id=1, replica_groups=mesh['dp'=8,'z'=8,'x'=4,'c'=2] {'z','x'}, dimensions={0} | all-to-all | bytes 1048576 | tf_op jit(solution)/shard_map/all_to_all | solution.py:35
  85.3 1.9 %fusion.28 = f32[32,32,128]{2,1,0:T(8,128)S(1)} fusion(f32[32,32,128]{2,1,0:T(8,128)S(1)} %all_to_all.16), kind=kOutput, calls=%fused_computation.37 | output fusion | flops 4063232 | bytes 1048576 | tf_op jit(solution)/shard_map/jit(cumsum)/reduce_window_sum | solution.py:16
  87.3 20.1 %all_to_all.17 = f32[32,32,128]{2,1,0:T(8,128)} all-to-all(f32[32,32,128]{2,1,0:T(8,128)S(1)} %concatenate.9), channel_id=1, replica_groups=mesh['dp'=8,'z'=8,'x'=4,'c'=2] {'z','x'}, dimensions={0} | all-to-all | bytes 1048576 | tf_op jit(solution)/shard_map/all_to_all | solution.py:37
  107.3 5.5 %collective-permute-start.1 = (f32[8,128,128]{2,1,0:T(8,128)}, f32[8,128,128]{2,1,0:T(8,128)S(1)}, u32[]{:S(2)}, u32[]{:S(2)}) collective-permute-start(f32[8,128,128]{2,1,0:T(8,128)} %bitcast.3), channel_id=1, source_target_pairs={{0,1},{1,0},{2,3},{3,2},{4,5},{5,4},{6,7},{7,6},{8,9},{9,8},{10,11... | collective-permute-start | bytes 1572872 | tf_op jit(solution)/shard_map/ppermute | solution.py:21
  112.8 1.2 copy.31
  114.7 0.0 copy-done.3
  114.7 0.1 mul.49
  114.8 0.0 copy-done
  114.8 0.6 convolution_bitcast_fusion
  115.5 0.0 collective-permute-done.1
  115.5 2.7 %fusion.9 = (f32[128,16]{0,1:T(8,128)S(1)}, f32[16,128,128]{2,1,0:T(8,128)S(1)}) fusion(f32[16,128,128]{2,1,0:T(8,128)S(1)} %convolution_bitcast_fusion, bf16[128,16,128]{2,1,0:T(8,128)(2,1)S(1)} %bitcast.43, f32[8,128,128]{2,1,0:T(8,128)S(1)} %collective-permute-done.1, f32[8,128,128]{2,1,0:T(8,128)} %bitcast.3, f32[16,128,128]{2,1,0:T(8,128)} %copy-done, ...), kind=kOutput, calls=%fused_computation.14 | convolution fusion | flops 404748288 | bytes 4726786 | tf_op jit(solution)/shard_map/nthd,nhde->nthe/dot_general | solution.py:74
  118.2 0.3 fusion.12
  118.6 0.0 all-gather.2.cloned.1.call-done
  118.6 5.5 %fusion = bf16[1,128,2048]{2,1,0:T(8,128)(2,1)} fusion(bf16[128,2048]{0,1:T(8,128)(2,1)S(1)} %bitcast.44, bf16[2048,2048]{1,0:T(8,128)(2,1)} %all-gather.2.cloned.1.call-done), kind=kOutput, calls=%fused_computation.1 | convolution fusion | flops 1074003968 | bytes 9437184 | tf_op jit(solution)/shard_map/dot_general | solution.py:92
  (8 shorter events, 0.1 us)
Async XLA Ops:
  6.5 47.4 %copy-start.1 = (bf16[1,128,2048]{2,1,0:T(8,128)(2,1)S(1)}, bf16[1,128,2048]{2,1,0:T(8,128)(2,1)}, u32[]{:S(2)}) copy-start(bf16[1,128,2048]{2,1,0:T(8,128)(2,1)} %param.7) | copy-start | bytes 1572868
  6.5 47.6 %copy-start.2 = (bf16[1,128,2048]{2,1,0:T(8,128)(2,1)S(1)}, bf16[1,128,2048]{2,1,0:T(8,128)(2,1)}, u32[]{:S(2)}) copy-start(bf16[1,128,2048]{2,1,0:T(8,128)(2,1)} %param.8) | copy-start | bytes 1572868
  6.5 112.1 %all-gather.2.cloned.1.call-start = ((), (), s32[]{:S(2)}) async-start(), calls=%async_computation.3 | async-start | bytes 9437184 | tf_op jit(solution)/shard_map/all_gather | solution.py:89
  51.9 62.8 %copy-start.3 = (f32[2048]{0:T(1024)S(1)}, f32[2048]{0:T(1024)}, u32[]{:S(2)}) copy-start(f32[2048]{0:T(1024)} %param.10) | copy-start | bytes 24580
  54.6 7.4 %collective-permute-start = (f32[16,128,128]{2,1,0:T(8,128)S(1)}, f32[16,128,128]{2,1,0:T(8,128)S(1)}, u32[]{:S(2)}, u32[]{:S(2)}) collective-permute-start(f32[16,128,128]{2,1,0:T(8,128)S(1)} %fusion.20), channel_id=1, source_target_pairs={{0,1},{1,0},{2,3},{3,2},{4,5},{5,4},{6,7},{7,6},{8,9},{9,8},{10,11... | collective-permute-start | bytes 3145736 | tf_op jit(solution)/shard_map/ppermute | solution.py:21
  62.0 52.8 %copy-start = (f32[16,128,128]{2,1,0:T(8,128)}, f32[16,128,128]{2,1,0:T(8,128)S(1)}, u32[]{:S(2)}) copy-start(f32[16,128,128]{2,1,0:T(8,128)S(1)} %collective-permute-done) | copy-start | bytes 3145732
  107.3 8.1 %collective-permute-start.1 = (f32[8,128,128]{2,1,0:T(8,128)}, f32[8,128,128]{2,1,0:T(8,128)S(1)}, u32[]{:S(2)}, u32[]{:S(2)}) collective-permute-start(f32[8,128,128]{2,1,0:T(8,128)} %bitcast.3), channel_id=1, source_target_pairs={{0,1},{1,0},{2,3},{3,2},{4,5},{5,4},{6,7},{7,6},{8,9},{9,8},{10,11... | collective-permute-start | bytes 1572872 | tf_op jit(solution)/shard_map/ppermute | solution.py:21
Sparse Core Ops, SparseCore 0:
  54.0 63.7 all-gather.1

commit v8 on v4

--- a/solution.py
+++ b/solution.py
@@ -22,19 +22,22 @@
 
 
 def prefix_of(own):
-    ci = lax.axis_index("c")
+    xi, ci = lax.axis_index("x"), lax.axis_index("c")
     nz, nx, nc = (lax.axis_size(a) for a in SEQ_AXES)
     assert nc == 2
     partner = swap_cores(own)
     chip_total = own + partner
     within_chip = jnp.where(ci == 1, partner, jnp.zeros_like(partner))
     half = HEADS // nc
-    chips = nz * nx
+    quarter = half // nx
     mine = lax.dynamic_slice_in_dim(chip_total, ci * half, half, 0)
-    pieces = mine.reshape(chips, half * HEAD // chips, HEAD)
-    by_chip = lax.all_to_all(pieces, ("z", "x"), 0, 0)
-    before, _ = exclusive_cumsum(by_chip)
-    back = lax.all_to_all(before, ("z", "x"), 0, 0)
+    by_chip = lax.all_to_all(mine.reshape(nx, quarter, HEAD, HEAD), "x", 0, 0)
+    before_in_row, row_total = exclusive_cumsum(by_chip)
+    pieces = row_total.reshape(nz, quarter * HEAD // nz, HEAD)
+    by_row = lax.all_to_all(pieces, "z", 0, 0)
+    before_rows, _ = exclusive_cumsum(by_row)
+    before_rows = lax.all_to_all(before_rows, "z", 0, 0).reshape(quarter, HEAD, HEAD)
+    back = lax.all_to_all(before_in_row + before_rows[None], "x", 0, 0)
     mine = back.reshape(half, HEAD, HEAD)
     theirs = swap_cores(mine)
     chip_prefix = jnp.where(

time: 129 us -> 130 us (level)
  starting transfers between devices: 10.4 us -> 14.3 us
  blocking collectives: 66.8 us -> 64.5 us
  other arithmetic: 2.35 us -> 0.97 us
    all_to_all x0 -> x1, waiting for transfers between devices: none -> 7.9 us  [prefix_of(): lax.all_to_all(before_rows, 'z', 0, 0).reshape(quarter, HEAD, HEAD)]
    all_gather x1, waiting for transfers between devices: 17.8 us -> 10.1 us  [body(): weight = lax.all_gather(wide, SEQ_AXES, axis=0, tiled=True)]
    all_to_all x0 -> x1, starting transfers between devices: none -> 3.37 us  [prefix_of(): lax.all_to_all(before_rows, 'z', 0, 0).reshape(quarter, HEAD, HEAD)]
    all_to_all x2 -> x3, blocking collectives: 51.5 us -> 49.2 us  [the longest x1 19.4 us: prefix_of(): by_row = lax.all_to_all(pieces, 'z', 0, 0)]
    another operation x1 -> x2, other arithmetic: 1.92 us -> 0.51 us  [exclusive_cumsum(): running = jnp.cumsum(stack, axis=0)]
  transfers between devices with their start and end apart: 3 -> 4, of which waited for: 2 -> 3; matrix products, arithmetic and copies ran while one was open for 8% -> 7% of each run, Pallas kernels for 0% -> 0%
where the time goes in v8:
time: 130 us; the launch traced here: 129 us
  blocking collectives  64.5 us (50%)
  waiting for transfers between devices  20.2 us (16%)
  starting transfers between devices  14.3 us (11%)
  between operations  14.2 us (11%)
  matrix products  9.08 us (7%)
  local copies, waits for them, and re-layouts  5.72 us (4%)
    all_to_all x1, blocking collectives, prefix_of(): by_row = lax.all_to_all(pieces, 'z', 0, 0)  19.4 us
    all_to_all x1, blocking collectives, prefix_of(): back = lax.all_to_all(before_in_row + before_rows[None], 'x', 0, 0)  17.4 us
    all_to_all x1, blocking collectives, body(): by_column = lax.all_to_all(copies, 'dp', 0, 0)  15.4 us
    all_to_all x1, blocking collectives, prefix_of(): by_chip = lax.all_to_all(mine.reshape(nx, quarter, HEAD, HEAD), 'x', 0, 0)  12.4 us
    ppermute x2, starting transfers between devices, swap_cores(): return lax.ppermute(x, 'c', [(0, 1), (1, 0)])  10.9 us
    all_gather x1, waiting for transfers between devices, body(): weight = lax.all_gather(wide, SEQ_AXES, axis=0, tiled=True)  10.1 us
    all_to_all x1, waiting for transfers between devices, prefix_of(): lax.all_to_all(before_rows, 'z', 0, 0).reshape(quarter, HEAD, HEAD)  7.9 us
    dot_general x1, matrix products, body(): result = jnp.dot(normed, weight, preferred_element_type=jnp.float32)  5.46 us
  transfers between devices with their start and end apart: 4, of which 3 were waited for; matrix products, arithmetic and copies ran while one was open for 7% of the time, Pallas kernels for 0%

profile of v8, /device:TPU:1, one launch (start us, length us, event | category | flops | bytes accessed | tf_op | source)
XLA Modules:
  0.0 129.0 jit_solution(16419922548550926258)
XLA Ops:
  6.5 0.0 all-gather.2.cloned.1.call-start
  6.5 0.7 broadcast_in_dim.46
  7.3 15.4 %all_to_all.25 = bf16[8,32,256]{2,1,0:T(8,128)(2,1)S(1)} all-to-all(bf16[8,32,256]{2,1,0:T(8,128)(2,1)S(1)} %broadcast_in_dim.46), channel_id=1, replica_groups=mesh['dp'=8,'z'=8,'x'=4,'c'=2] {'dp'}, dimensions={0} | all-to-all | bytes 262144 | tf_op jit(solution)/shard_map/all_to_all | solution.py:90
  22.6 0.7 copy.27
  23.3 0.0 all-gather.2.cloned.1.call-update
  23.3 1.3 %copy.26 = bf16[1,128,2048]{1,2,0:T(8,128)(2,1)S(1)} copy(bf16[1,128,2048]{2,1,0:T(8,128)(2,1)} %param.7) | data formatting | bytes 1048576 | tf_op jit(solution)/shard_map/reshape.2
  24.6 1.1 copy.29
  25.8 0.3 fusion.20
  26.1 0.0 copy-start.1
  26.1 4.8 %collective-permute-start = (f32[16,128,128]{2,1,0:T(8,128)S(1)}, f32[16,128,128]{2,1,0:T(8,128)S(1)}, u32[]{:S(2)}, u32[]{:S(2)}) collective-permute-start(f32[16,128,128]{2,1,0:T(8,128)S(1)} %fusion.20), channel_id=1, source_target_pairs={{0,1},{1,0},{2,3},{3,2},{4,5},{5,4},{6,7},{7,6},{8,9},{9,8},{10,11... | collective-permute-start | bytes 3145736 | tf_op jit(solution)/shard_map/ppermute | solution.py:21
  31.0 2.3 %collective-permute-done = f32[16,128,128]{2,1,0:T(8,128)S(1)} collective-permute-done((f32[16,128,128]{2,1,0:T(8,128)S(1)}, f32[16,128,128]{2,1,0:T(8,128)S(1)}, u32[]{:S(2)}, u32[]{:S(2)}) %collective-permute-start) | collective-permute-done | bytes 1048608 | tf_op jit(solution)/shard_map/ppermute | solution.py:21
  33.2 0.0 copy-start
  33.2 0.1 dynamic-slice_add_fusion
  33.3 12.4 %all_to_all.26 = f32[4,2,128,128]{3,2,1,0:T(8,128)S(1)} all-to-all(f32[4,2,128,128]{3,2,1,0:T(8,128)S(1)} %bitcast.49), channel_id=1, replica_groups=mesh['dp'=8,'z'=8,'x'=4,'c'=2] {'x'}, dimensions={0} | all-to-all | bytes 1048576 | tf_op jit(solution)/shard_map/all_to_all | solution.py:34
  45.7 0.3 fusion.28
  46.0 19.4 %all_to_all.27 = f32[8,32,128]{2,1,0:T(8,128)S(1)} all-to-all(f32[8,32,128]{2,1,0:T(8,128)S(1)} %bitcast.54), channel_id=1, replica_groups=mesh['dp'=8,'z'=8,'x'=4,'c'=2] {'z'}, dimensions={0} | all-to-all | bytes 262144 | tf_op jit(solution)/shard_map/all_to_all | solution.py:37
  65.4 0.2 fusion.29
  65.6 0.7 concatenate.13
  66.3 3.4 %all-to-all-start.2 = ((f32[8,32,128]{2,1,0:T(8,128)}), f32[8,32,128]{2,1,0:T(8,128)S(1)}, u32[]{:S(2)}, u32[]{:S(2)}) async-start(f32[8,32,128]{2,1,0:T(8,128)} %concatenate.13), calls=%async_computation.2 | async-start | bytes 262144 | tf_op jit(solution)/shard_map/all_to_all | solution.py:39
  69.7 7.9 %all-to-all-done.2 = f32[8,32,128]{2,1,0:T(8,128)S(1)} async-done(((f32[8,32,128]{2,1,0:T(8,128)}), f32[8,32,128]{2,1,0:T(8,128)S(1)}, u32[]{:S(2)}, u32[]{:S(2)}) %all-to-all-start.2) | async-done | bytes 131104 | tf_op jit(solution)/shard_map/all_to_all | solution.py:39
  77.6 17.4 %all_to_all.28 = f32[4,2,128,128]{3,2,1,0:T(8,128)} all-to-all(f32[4,2,128,128]{3,2,1,0:T(8,128)S(1)} %pad_add_fusion), channel_id=1, replica_groups=mesh['dp'=8,'z'=8,'x'=4,'c'=2] {'x'}, dimensions={0} | all-to-all | bytes 1048576 | tf_op jit(solution)/shard_map/all_to_all | solution.py:40
  95.0 6.1 %collective-permute-start.1 = (f32[8,128,128]{2,1,0:T(8,128)}, f32[8,128,128]{2,1,0:T(8,128)S(1)}, u32[]{:S(2)}, u32[]{:S(2)}) collective-permute-start(f32[8,128,128]{2,1,0:T(8,128)} %bitcast.5), channel_id=1, source_target_pairs={{0,1},{1,0},{2,3},{3,2},{4,5},{5,4},{6,7},{7,6},{8,9},{9,8},{10,11... | collective-permute-start | bytes 1572872 | tf_op jit(solution)/shard_map/ppermute | solution.py:21
  101.1 1.1 copy.28
  103.0 0.0 copy-done
  103.0 0.6 convolution_bitcast_fusion
  103.6 0.0 collective-permute-done.1
  103.6 2.7 %fusion.12 = (f32[128,16]{0,1:T(8,128)S(1)}, f32[16,128,128]{2,1,0:T(8,128)S(1)}) fusion(f32[16,128,128]{2,1,0:T(8,128)S(1)} %convolution_bitcast_fusion, bf16[128,16,128]{2,1,0:T(8,128)(2,1)S(1)} %bitcast.48, f32[8,128,128]{2,1,0:T(8,128)S(1)} %collective-permute-done.1, f32[8,128,128]{2,1,0:T(8,128)} %bitcast.5, f32[16,128,128]{2,1,0:T(8,128)} %copy-done, ...), kind=kOutput, calls=%fused_computation.18 | convolution fusion | flops 404748288 | bytes 4726786 | tf_op jit(solution)/shard_map/nthd,nhde->nthe/dot_general | solution.py:77
  106.3 0.0 copy-done.1
  106.3 0.3 fusion.11
  106.7 10.1 %all-gather.2.cloned.1.call-done = bf16[2048,2048]{1,0:T(8,128)(2,1)} async-done(((bf16[32,2048]{1,0:T(8,128)(2,1)}), bf16[2048,2048]{1,0:T(8,128)(2,1)}) %all-gather.2.cloned.1.call-update) | async-done | bytes 8388624 | tf_op jit(solution)/shard_map/all_gather | solution.py:92
  116.7 5.5 %fusion = bf16[1,128,2048]{2,1,0:T(8,128)(2,1)} fusion(bf16[128,2048]{0,1:T(8,128)(2,1)S(1)} %fusion.11, bf16[2048,2048]{1,0:T(8,128)(2,1)} %all-gather.2.cloned.1.call-done), kind=kOutput, calls=%fused_computation.1 | convolution fusion | flops 1074003968 | bytes 9437184 | tf_op jit(solution)/shard_map/dot_general | solution.py:94
  (7 shorter events, 0.1 us)
Async XLA Ops:
  6.5 110.2 %all-gather.2.cloned.1.call-start = ((), (), s32[]{:S(2)}) async-start(), calls=%async_computation.5 | async-start | bytes 8519680 | tf_op jit(solution)/shard_map/all_gather | solution.py:92
  26.1 80.2 %copy-start.1 = (f32[2048]{0:T(1024)S(1)}, f32[2048]{0:T(1024)}, u32[]{:S(2)}) copy-start(f32[2048]{0:T(1024)} %param.10) | copy-start | bytes 24580
  26.1 7.1 %collective-permute-start = (f32[16,128,128]{2,1,0:T(8,128)S(1)}, f32[16,128,128]{2,1,0:T(8,128)S(1)}, u32[]{:S(2)}, u32[]{:S(2)}) collective-permute-start(f32[16,128,128]{2,1,0:T(8,128)S(1)} %fusion.20), channel_id=1, source_target_pairs={{0,1},{1,0},{2,3},{3,2},{4,5},{5,4},{6,7},{7,6},{8,9},{9,8},{10,11... | collective-permute-start | bytes 3145736 | tf_op jit(solution)/shard_map/ppermute | solution.py:21
  33.2 69.8 %copy-start = (f32[16,128,128]{2,1,0:T(8,128)}, f32[16,128,128]{2,1,0:T(8,128)S(1)}, u32[]{:S(2)}) copy-start(f32[16,128,128]{2,1,0:T(8,128)S(1)} %collective-permute-done) | copy-start | bytes 3145732
  66.3 11.3 %all-to-all-start.2 = ((f32[8,32,128]{2,1,0:T(8,128)}), f32[8,32,128]{2,1,0:T(8,128)S(1)}, u32[]{:S(2)}, u32[]{:S(2)}) async-start(f32[8,32,128]{2,1,0:T(8,128)} %concatenate.13), calls=%async_computation.2 | async-start | bytes 262144 | tf_op jit(solution)/shard_map/all_to_all | solution.py:39
  95.0 8.6 %collective-permute-start.1 = (f32[8,128,128]{2,1,0:T(8,128)}, f32[8,128,128]{2,1,0:T(8,128)S(1)}, u32[]{:S(2)}, u32[]{:S(2)}) collective-permute-start(f32[8,128,128]{2,1,0:T(8,128)} %bitcast.5), channel_id=1, source_target_pairs={{0,1},{1,0},{2,3},{3,2},{4,5},{5,4},{6,7},{7,6},{8,9},{9,8},{10,11... | collective-permute-start | bytes 1572872 | tf_op jit(solution)/shard_map/ppermute | solution.py:21
Sparse Core Ops, SparseCore 0:
  23.4 93.2 all-gather.1
